TPU v7x, 512 devices: a whole 4x8x8 slice. The times are simulated.
512 devices in a mesh: fsdp: 16 (over y, core), expert: 32 (over x, z).
Axes of the slice: x: 4, y: 8, z: 8, core: 2. Of those that a mesh axis runs over, the one named last changes fastest.
Arguments:
- frames: bfloat16 [16, 4096, 1536], P('fsdp', 'expert'), may hold values from -6 to 6
- ln_gain: float32 [1536], replicated, may hold values from 0.5 to 1.5
- kernel: float32 [31, 1536], replicated, may hold values from -1 to 1
- bn_scale: float32 [1536], replicated, may hold values from 0.5 to 2
- bn_shift: float32 [1536], replicated, may hold values from -1 to 1
- ffn_gain: float32 [1536], replicated, may hold values from 0.5 to 1.5
- expert_ids: int32 [16, 4096, 2], P('fsdp', 'expert'), may hold values from 0 to 31, all different within a row; in each aligned block of 128 rows (0 to 127, 128 to 255, ..., all dimensions but the last counted through in order) at most 16 rows name the same one
- gates: float32 [16, 4096, 2], P('fsdp', 'expert'), may hold values from 0.1 to 1
- w_in: bfloat16 [32, 1536, 1536], P('expert', 'fsdp'), may hold values from -0.15625 to 0.15625
- w_out: bfloat16 [32, 1536, 1536], P('expert', 'fsdp'), may hold values from -0.15625 to 0.15625
Outputs:
- layer_out: bfloat16 [16, 4096, 1536], P('fsdp', 'expert')
Inputs may be any that keep to these rules, and one draw needn't show every extreme that they name: `expert_ids`: the 2 experts of a frame differ; within the 128 frames of one device (aligned blocks along a sequence) no expert is named more than 16 times, a bound that some block reaches.
All inputs are finite; a program needn't handle non-finite values.
Results may differ from a plain program's by a relative error of at most 0.0039.
Values may be sent and summed in bfloat16 or wider, within the bound.
No kernel may reach another device: no remote copies, remote signals or barrier semaphores. Data moves between devices by JAX's collectives and lax.ppermute only.
A program may use at most 64 MiB of HBM per device.

v0:
```python
import jax
import jax.numpy as jnp
from jax import lax
from jax.sharding import PartitionSpec as P

eps_norm = 1e-05


def padded_2(block, sides, width):
    for axis, dim in sides:
        count = lax.axis_size(axis)
        forward = [(i, i + 1) for i in range(count - 1)]
        backward = [(target, source) for source, target in forward]
        low = lax.ppermute(
            lax.slice_in_dim(block, block.shape[dim] - width, None, axis=dim), axis, forward
        )
        high = lax.ppermute(lax.slice_in_dim(block, 0, width, axis=dim), axis, backward)
        block = jnp.concatenate([low, block, high], axis=dim)
    return block


def layer_norm(values, gain):
    centre = jnp.mean(values, axis=-1, keepdims=True)
    centred = values - centre
    spread = jnp.mean(centred * centred, axis=-1, keepdims=True)
    return centred * lax.rsqrt(spread + eps_norm) * gain


def shards(frames, ln_gain, kernel, bn_scale, bn_shift, ffn_gain, expert_ids, gates, w_in, w_out):
    frame_count = frames.shape[1]
    width = frames.shape[2]
    taps = kernel.shape[0]
    reach = (taps - 1) // 2
    picks_per = expert_ids.shape[2]
    experts_all = lax.axis_size("expert") * w_in.shape[0]
    capacity = 2 * picks_per * frame_count // experts_all
    slots_all = experts_all * capacity
    stream = frames[0].astype(jnp.float32)
    normed = layer_norm(stream, ln_gain).astype(jnp.bfloat16)
    padded = padded_2(normed, (("expert", 0),), reach)
    filtered = jnp.zeros(stream.shape, jnp.float32)
    for offset in range(taps):
        filtered = filtered + kernel[offset] * padded[offset : offset + frame_count]
    mixed = stream + jax.nn.silu(bn_scale * filtered + bn_shift)
    routed = layer_norm(mixed, ffn_gain).astype(jnp.bfloat16)
    chosen = expert_ids[0].reshape(-1)
    onehot = (chosen[:, None] == jnp.arange(experts_all, dtype=jnp.int32)[None, :]).astype(
        jnp.int32
    )
    before = jnp.cumsum(onehot, axis=0) - onehot
    slot_at = jnp.sum(before * onehot, axis=1)
    target = (chosen * capacity + slot_at).reshape(frame_count, picks_per)
    placing = jnp.any(
        target[None, :, :] == jnp.arange(slots_all, dtype=jnp.int32)[:, None, None], axis=2
    )
    outgoing = jnp.dot(placing.astype(jnp.bfloat16), routed, preferred_element_type=jnp.float32)
    outgoing = outgoing.astype(jnp.bfloat16).reshape(experts_all, capacity, width)
    full_in, full_out = (
        lax.all_gather(w_in, "fsdp", axis=1, tiled=True),
        lax.all_gather(w_out, "fsdp", axis=1, tiled=True),
    )
    block = lax.all_to_all(outgoing, "expert", split_axis=0, concat_axis=0, tiled=True)
    rows_in = block.reshape(-1, width)
    hidden = jax.nn.silu(jnp.dot(rows_in, full_in[0], preferred_element_type=jnp.float32)).astype(
        jnp.bfloat16
    )
    result = jnp.dot(hidden, full_out[0], preferred_element_type=jnp.float32).astype(jnp.bfloat16)
    returned = lax.all_to_all(
        result.reshape(block.shape), "expert", split_axis=0, concat_axis=0, tiled=True
    )
    rows_back = returned.reshape(-1, width)
    picked = (
        jnp.take(rows_back, target.reshape(-1), axis=0)
        .reshape(frame_count, picks_per, width)
        .astype(jnp.float32)
    )
    combined = jnp.sum(gates[0][:, :, None] * picked, axis=1)
    return (mixed + 0.5 * combined).astype(jnp.bfloat16)[None]


def solution(mesh):
    return jax.shard_map(
        shards,
        mesh=mesh,
        in_specs=(
            P("fsdp", "expert", None),
            P(),
            P(),
            P(),
            P(),
            P(),
            P("fsdp", "expert", None),
            P("fsdp", "expert", None),
            P("expert", "fsdp", None),
            P("expert", "fsdp", None),
        ),
        out_specs=P("fsdp", "expert", None),
        check_vma=False,
    )
```

profile of v0, /device:TPU:8, one launch (start us, length us, event | category | flops | bytes accessed | tf_op | source)
XLA Modules:
  0.0 176.9 jit_solution(17045224739113966874)
XLA Ops:
  6.5 0.0 copy-start
  6.5 0.0 copy-start.1
  6.5 0.0 copy-start.3
  6.5 0.0 copy-start.2
  6.5 0.0 copy-start.4
  6.5 0.0 all-gather.3.cloned.1.call-start
  6.6 0.7 all-gather.3.cloned.1.call-update
  7.3 0.0 all-gather.5.cloned.1.call-start
  7.3 0.7 all-gather.5.cloned.1.call-update
  8.0 1.1 convert_reduce_fusion
  9.2 1.2 fusion.15
  10.4 1.3 fusion.17
  11.7 4.3 %collective-permute-start = (bf16[15,1536]{1,0:T(8,128)(2,1)S(1)}, bf16[15,1536]{1,0:T(8,128)(2,1)S(1)}, u32[]{:S(2)}, u32[]{:S(2)}) collective-permute-start(bf16[15,1536]{1,0:T(8,128)(2,1)S(1)} %get-tuple-element.38), channel_id=1, source_target_pairs={{0,1},{1,2},{2,3},{3,4},{4,5},{5,6},{6,7},{7,8},{8,9},{9,10},{10,1... | collective-permute-start | bytes 138248 | tf_op jit(solution)/shard_map/ppermute | solution.py:14
  16.0 1.3 collective-permute-start.1
  17.3 0.8 copy.26
  18.1 0.1 eq.41
  18.3 0.1 reshape_squeeze.3
  18.4 0.6 reduce-window.6
  19.0 0.2 slice_reduce_fusion
  19.2 0.1 fusion.53
  19.3 0.1 reduce_sum.64
  19.5 0.1 copy.31
  19.5 1.4 slice_reduce_fusion.30
  21.0 1.9 %slice_reduce_fusion.31 = (f32[1536]{0:T(1024)S(1)}, f32[1536]{0:T(1024)S(1)}, f32[1536]{0:T(1024)S(1)}, f32[1536]{0:T(1024)S(1)}, f32[1536]{0:T(1024)S(1)}, /*i...) fusion(f32[31,1536]{1,0:T(8,128)} %param.12), kind=kLoop, calls=%fused_computation.145 | loop fusion | bytes 233472 | tf_op jit(solution)/shard_map/slice | solution.py:43
  22.8 0.0 copy-done.1
  22.9 0.1 fusion.18
  22.9 0.0 collective-permute-done
  22.9 0.0 collective-permute-done.1
  23.0 0.0 copy-done
  23.0 0.0 copy-done.3
  23.0 0.0 copy-done.2
  23.0 4.3 %fusion.56 = (f32[128]{0:T(128)S(1)}, f32[128,1536]{1,0:T(8,128)S(1)}) fusion(f32[1536]{0:T(1024)S(1)} %copy-done.2, bf16[15,1536]{1,0:T(8,128)(2,1)S(1)} %collective-permute-done.1, bf16[128,1536]{1,0:T(8,128)(2,1)S(1)} %fusion.17, f32[1536]{0:T(1024)S(1)} %get-tuple-element.34, f32[1536]{0:T(1024)S(1)} %get-tuple-element.35, ...), kind=kLoop, calls=%fused_computation.158 | loop fusion | flops 37552000 | bytes 1868288 | tf_op jit(solution)/shard_map/reduce_sum | solution.py:23
  27.4 0.2 multiply_reduce_fusion.1
  27.6 0.0 copy-done.4
  27.6 0.7 convolution_convert_fusion
  28.3 54.0 %all_to_all.10 = bf16[32,16,1536]{2,1,0:T(8,128)(2,1)S(1)} all-to-all(bf16[32,16,1536]{2,1,0:T(8,128)(2,1)S(1)} %bitcast.66), channel_id=1, replica_groups=mesh['fsdp'=16,'expert'=32] {'expert'}, dimensions={0} | all-to-all | bytes 3145728 | tf_op jit(solution)/shard_map/all_to_all | solution.py:62
  82.2 0.0 all-gather.3.cloned.1.call-done
  82.2 21.9 %all-gather.5.cloned.1.call-done = bf16[1,1536,1536]{2,1,0:T(8,128)(2,1)} async-done(((bf16[1,96,1536]{2,1,0:T(8,128)(2,1)}), bf16[1,1536,1536]{2,1,0:T(8,128)(2,1)}) %all-gather.5.cloned.1.call-update) | async-done | bytes 4718608 | tf_op jit(solution)/shard_map/all_gather | solution.py:60
  104.1 10.3 %fusion.4 = bf16[512,1536]{1,0:T(8,128)(2,1)} fusion(bf16[1,1536,1536]{2,1,0:T(8,128)(2,1)} %all-gather.5.cloned.1.call-done, bf16[512,1536]{1,0:T(8,128)(2,1)S(1)} %bitcast.68, bf16[1,1536,1536]{2,1,0:T(8,128)(2,1)} %all-gather.3.cloned.1.call-done), kind=kOutput, calls=%fused_computation.6 | convolution fusion | flops 4836556800 | bytes 12582912 | tf_op jit(solution)/shard_map/dot_general | solution.py:67
  114.4 0.0 copy-start.5
  114.4 10.5 %all-to-all-start.1 = ((bf16[32,16,1536]{2,1,0:T(8,128)(2,1)}), bf16[32,16,1536]{2,1,0:T(8,128)(2,1)S(1)}, u32[]{:S(2)}, u32[]{:S(2)}) async-start(bf16[32,16,1536]{2,1,0:T(8,128)(2,1)} %bitcast.67), calls=%async_computation.1 | async-start | bytes 3145728 | tf_op jit(solution)/shard_map/all_to_all | solution.py:68
  124.9 0.1 reduce_sum.63
  125.0 0.1 copy.32
  125.1 0.1 mul.519
  125.3 0.1 copy.29
  125.4 0.1 copy.30
  125.5 0.0 copy-done.5
  125.5 0.1 copy.25
  125.7 38.9 %all-to-all-done.1 = bf16[32,16,1536]{2,1,0:T(8,128)(2,1)S(1)} async-done(((bf16[32,16,1536]{2,1,0:T(8,128)(2,1)}), bf16[32,16,1536]{2,1,0:T(8,128)(2,1)S(1)}, u32[]{:S(2)}, u32[]{:S(2)}) %all-to-all-start.1) | async-done | bytes 1572896 | tf_op jit(solution)/shard_map/all_to_all | solution.py:68
  164.5 1.3 gather_fusion
  165.8 0.3 gather.7
  166.1 3.1 %multiply_reduce_fusion = f32[128,1536]{1,0:T(8,128)S(1)} fusion(bf16[128,2,1536]{2,1,0:T(2,128)(2,1)S(1)} %gather.7, pred[128,2]{1,0:T(8,128)(4,1)S(1)} %copy.30, f32[128,2]{1,0:T(8,128)S(1)} %copy.25), kind=kLoop, calls=%fused_computation.36 | loop fusion | flops 1376256 | bytes 1574144 | tf_op jit(solution)/shard_map/reduce_sum | solution.py:77
  169.2 0.8 fusion.19
  (12 shorter events, 0.1 us)
Async XLA Ops:
  6.5 16.4 %copy-start = (bf16[1,128,1536]{2,1,0:T(8,128)(2,1)S(1)}, bf16[1,128,1536]{2,1,0:T(8,128)(2,1)}, u32[]{:S(2)}) copy-start(bf16[1,128,1536]{2,1,0:T(8,128)(2,1)} %param.10) | copy-start | bytes 1179652
  6.5 16.3 %copy-start.1 = (s32[1,128,2]{1,2,0:T(2,128)S(1)}, s32[1,128,2]{1,2,0:T(2,128)}, u32[]{:S(2)}) copy-start(s32[1,128,2]{1,2,0:T(2,128)} %param.16) | copy-start | bytes 3076
  6.5 16.4 %copy-start.3 = (f32[1536]{0:T(1024)S(1)}, f32[1536]{0:T(1024)}, u32[]{:S(2)}) copy-start(f32[1536]{0:T(1024)} %param.13) | copy-start | bytes 18436
  6.5 16.4 %copy-start.2 = (f32[1536]{0:T(1024)S(1)}, f32[1536]{0:T(1024)}, u32[]{:S(2)}) copy-start(f32[1536]{0:T(1024)} %param.14) | copy-start | bytes 18436
  6.5 21.0 %copy-start.4 = (f32[1536]{0:T(1024)S(1)}, f32[1536]{0:T(1024)}, u32[]{:S(2)}) copy-start(f32[1536]{0:T(1024)} %param.15) | copy-start | bytes 18436
  6.5 75.7 %all-gather.3.cloned.1.call-start = ((), (), s32[]{:S(2)}) async-start(), calls=%async_computation.2 | async-start | bytes 5013504 | tf_op jit(solution)/shard_map/all_gather | solution.py:59
  7.3 96.8 %all-gather.5.cloned.1.call-start = ((), (), s32[]{:S(2)}) async-start(), calls=%async_computation.3 | async-start | bytes 5013504 | tf_op jit(solution)/shard_map/all_gather | solution.py:60
  11.7 11.2 %collective-permute-start = (bf16[15,1536]{1,0:T(8,128)(2,1)S(1)}, bf16[15,1536]{1,0:T(8,128)(2,1)S(1)}, u32[]{:S(2)}, u32[]{:S(2)}) collective-permute-start(bf16[15,1536]{1,0:T(8,128)(2,1)S(1)} %get-tuple-element.38), channel_id=1, source_target_pairs={{0,1},{1,2},{2,3},{3,4},{4,5},{5,6},{6,7},{7,8},{8,9},{9,10},{10,1... | collective-permute-start | bytes 138248 | tf_op jit(solution)/shard_map/ppermute | solution.py:14
  16.0 6.9 %collective-permute-start.1 = (bf16[15,1536]{1,0:T(8,128)(2,1)S(1)}, bf16[15,1536]{1,0:T(8,128)(2,1)S(1)}, u32[]{:S(2)}, u32[]{:S(2)}) collective-permute-start(bf16[15,1536]{1,0:T(8,128)(2,1)S(1)} %get-tuple-element.39), channel_id=1, source_target_pairs={{1,0},{2,1},{3,2},{4,3},{5,4},{6,5},{7,6},{8,7},{9,8},{10,9},{11,1... | collective-permute-start | bytes 138248 | tf_op jit(solution)/shard_map/ppermute | solution.py:17
  114.4 11.1 %copy-start.5 = (f32[1,128,2]{1,2,0:T(2,128)S(1)}, f32[1,128,2]{1,2,0:T(2,128)}, u32[]{:S(2)}) copy-start(f32[1,128,2]{1,2,0:T(2,128)} %param.17) | copy-start | bytes 3076
  114.4 50.1 %all-to-all-start.1 = ((bf16[32,16,1536]{2,1,0:T(8,128)(2,1)}), bf16[32,16,1536]{2,1,0:T(8,128)(2,1)S(1)}, u32[]{:S(2)}, u32[]{:S(2)}) async-start(bf16[32,16,1536]{2,1,0:T(8,128)(2,1)} %bitcast.67), calls=%async_computation.1 | async-start | bytes 3145728 | tf_op jit(solution)/shard_map/all_to_all | solution.py:68
Sparse Core Ops, SparseCore 0:
  9.5 48.9 all-gather.2
  60.5 43.5 all-gather.4
where the time goes:
time: 177 us
  waiting for transfers between devices  62.1 us (35%)
  blocking collectives  54 us (31%)
  starting transfers between devices  16.1 us (9%)
  between operations  13.6 us (8%)
  other arithmetic  13 us (7%)
  matrix products  10.9 us (6%)
  local copies, waits for them, and re-layouts  7.04 us (4%)
    all_to_all x1, blocking collectives, shards(): lax.all_to_all(outgoing, 'expert', split_axis=0, concat_axis=0, tiled=True)  54 us
    all_to_all x1, waiting for transfers between devices, shards(): lax.all_to_all(result.reshape(block.shape), 'expert', split_axis=0, conca...  38.9 us
    all_gather x1, waiting for transfers between devices, shards(): lax.all_gather(w_out, 'fsdp', axis=1, tiled=True)  21.9 us
    all_to_all x1, starting transfers between devices, shards(): lax.all_to_all(result.reshape(block.shape), 'expert', split_axis=0, conca...  10.5 us
    dot_general x1, matrix products, shards(): jnp.dot(hidden, full_out[0], preferred_element_type=jnp.float32)  10.3 us
    reduce_sum x2, other arithmetic, layer_norm(): centre = jnp.mean(values, axis=-1, keepdims=True)  5.48 us
    ppermute x1, starting transfers between devices, padded_2(): lax.ppermute(lax.slice_in_dim(block, block.shape[dim] - width, None, axis...  4.28 us
  transfers between devices with their start and end apart: 5, of which 2 were waited for; matrix products, arithmetic and copies ran while one was open for 9% of the time, Pallas kernels for 0%

commit v1 on v0

--- a/solution.py
+++ b/solution.py
@@ -55,26 +55,34 @@
     )
     outgoing = jnp.dot(placing.astype(jnp.bfloat16), routed, preferred_element_type=jnp.float32)
     outgoing = outgoing.astype(jnp.bfloat16).reshape(experts_all, capacity, width)
-    full_in, full_out = (
-        lax.all_gather(w_in, "fsdp", axis=1, tiled=True),
-        lax.all_gather(w_out, "fsdp", axis=1, tiled=True),
-    )
+    chunks = 2
+    piece = width // chunks
+    full_in = lax.all_gather(w_in, "fsdp", axis=1, tiled=True)
+    out_pieces = [
+        lax.all_gather(w_out[:, :, j * piece : (j + 1) * piece], "fsdp", axis=1, tiled=True)
+        for j in range(chunks)
+    ]
     block = lax.all_to_all(outgoing, "expert", split_axis=0, concat_axis=0, tiled=True)
     rows_in = block.reshape(-1, width)
     hidden = jax.nn.silu(jnp.dot(rows_in, full_in[0], preferred_element_type=jnp.float32)).astype(
         jnp.bfloat16
     )
-    result = jnp.dot(hidden, full_out[0], preferred_element_type=jnp.float32).astype(jnp.bfloat16)
-    returned = lax.all_to_all(
-        result.reshape(block.shape), "expert", split_axis=0, concat_axis=0, tiled=True
-    )
-    rows_back = returned.reshape(-1, width)
-    picked = (
-        jnp.take(rows_back, target.reshape(-1), axis=0)
-        .reshape(frame_count, picks_per, width)
-        .astype(jnp.float32)
-    )
-    combined = jnp.sum(gates[0][:, :, None] * picked, axis=1)
+    parts = []
+    for j in range(chunks):
+        result = jnp.dot(hidden, out_pieces[j][0], preferred_element_type=jnp.float32).astype(
+            jnp.bfloat16
+        )
+        returned = lax.all_to_all(
+            result.reshape(experts_all, capacity, piece), "expert", split_axis=0, concat_axis=0, tiled=True
+        )
+        rows_back = returned.reshape(-1, piece)
+        picked = (
+            jnp.take(rows_back, target.reshape(-1), axis=0)
+            .reshape(frame_count, picks_per, piece)
+            .astype(jnp.float32)
+        )
+        parts.append(jnp.sum(gates[0][:, :, None] * picked, axis=1))
+    combined = jnp.concatenate(parts, axis=1)
     return (mixed + 0.5 * combined).astype(jnp.bfloat16)[None]
 
 

time: 177 us -> 195 us (1.10)
  the two profiles are of different devices: /device:TPU:8 before, /device:TPU:64 now
where the time goes in v1:
time: 195 us; the launch traced here: 194 us
  waiting for transfers between devices  105 us (54%)
  starting transfers between devices  40.9 us (21%)
  matrix products  16.9 us (9%)
  between operations  13.3 us (7%)
  other arithmetic  12.3 us (6%)
  local copies, waits for them, and re-layouts  6.48 us (3%)
    all_gather x2, waiting for transfers between devices, shards(): lax.all_gather(w_out[:, :, j * piece:(j + 1) * piece], 'fsdp', axis=1, ti...  43.6 us
    all_to_all x1, waiting for transfers between devices, shards(): lax.all_to_all(outgoing, 'expert', split_axis=0, concat_axis=0, tiled=True)  37.3 us
    all_to_all x2, waiting for transfers between devices, shards(): lax.all_to_all(result.reshape(experts_all, capacity, piece), 'expert', sp...  22 us
    all_to_all x2, starting transfers between devices, shards(): lax.all_to_all(result.reshape(experts_all, capacity, piece), 'expert', sp...  20.6 us
    all_to_all x1, starting transfers between devices, shards(): lax.all_to_all(outgoing, 'expert', split_axis=0, concat_axis=0, tiled=True)  12 us
    dot_general x2, matrix products, shards(): jnp.dot(hidden, out_pieces[j][0], preferred_element_type=jnp.float32)  8.84 us
    dot_general x1, matrix products, shards(): jnp.dot(rows_in, full_in[0], preferred_element_type=jnp.float32)  6.22 us
    reduce_sum x2, other arithmetic, layer_norm(): centre = jnp.mean(values, axis=-1, keepdims=True)  5.48 us
  transfers between devices with their start and end apart: 8, of which 5 were waited for; matrix products, arithmetic and copies ran while one was open for 16% of the time, Pallas kernels for 0%

profile of v1, /device:TPU:64, one launch (start us, length us, event | category | flops | bytes accessed | tf_op | source)
XLA Modules:
  0.0 194.4 jit_solution(16616659230168677464)
XLA Ops:
  6.5 0.0 copy-start
  6.5 0.0 copy-start.5
  6.5 0.0 copy-start.1
  6.5 0.0 copy-start.3
  6.5 0.0 copy-start.2
  6.5 0.0 all-gather.4.cloned.1.call-start
  6.6 0.7 all-gather.4.cloned.1.call-update
  7.3 0.0 all-gather.6.cloned.1.call-start
  7.3 1.7 fusion.63
  9.0 0.0 all-gather.6.cloned.1.call-update
  9.1 1.1 convert_reduce_fusion
  10.2 1.2 fusion.18
  11.5 0.0 copy-start.4
  11.5 1.3 fusion.20
  12.8 4.3 %collective-permute-start = (bf16[15,1536]{1,0:T(8,128)(2,1)S(1)}, bf16[15,1536]{1,0:T(8,128)(2,1)S(1)}, u32[]{:S(2)}, u32[]{:S(2)}) collective-permute-start(bf16[15,1536]{1,0:T(8,128)(2,1)S(1)} %get-tuple-element.43), channel_id=1, source_target_pairs={{0,1},{1,2},{2,3},{3,4},{4,5},{5,6},{6,7},{7,8},{8,9},{9,10},{10,1... | collective-permute-start | bytes 138248 | tf_op jit(solution)/shard_map/ppermute | solution.py:14
  17.1 3.9 %collective-permute-start.1 = (bf16[15,1536]{1,0:T(8,128)(2,1)S(1)}, bf16[15,1536]{1,0:T(8,128)(2,1)S(1)}, u32[]{:S(2)}, u32[]{:S(2)}) collective-permute-start(bf16[15,1536]{1,0:T(8,128)(2,1)S(1)} %get-tuple-element.44), channel_id=1, source_target_pairs={{1,0},{2,1},{3,2},{4,3},{5,4},{6,5},{7,6},{8,7},{9,8},{10,9},{11,1... | collective-permute-start | bytes 138248 | tf_op jit(solution)/shard_map/ppermute | solution.py:17
  21.0 0.0 copy-done.5
  21.0 0.1 copy.27
  21.1 0.1 eq.44
  21.3 0.1 eq.40
  21.4 0.6 reduce-window.6
  22.0 0.2 slice_reduce_fusion
  22.2 0.1 fusion.58
  22.4 0.1 reduce_sum.68
  22.5 0.1 copy.30
  22.6 0.0 copy-done.1
  22.6 0.2 slice_reduce_fusion.30
  22.8 0.3 slice_reduce_fusion.31
  23.1 0.1 fusion.23
  23.2 0.0 collective-permute-done
  23.2 0.2 collective-permute-done.1
  23.4 0.0 copy-done
  23.4 0.0 copy-done.3
  23.4 0.0 copy-done.2
  23.4 4.3 %fusion.60 = (f32[128]{0:T(128)S(1)}, f32[128,1536]{1,0:T(8,128)S(1)}) fusion(f32[1536]{0:T(1024)S(1)} %copy-done.2, bf16[15,1536]{1,0:T(8,128)(2,1)S(1)} %collective-permute-done.1, bf16[128,1536]{1,0:T(8,128)(2,1)S(1)} %fusion.20, f32[1536]{0:T(1024)S(1)} %get-tuple-element.35, f32[1536]{0:T(1024)S(1)} %get-tuple-element.36, ...), kind=kLoop, calls=%fused_computation.162 | loop fusion | flops 37552000 | bytes 1868288 | tf_op jit(solution)/shard_map/reduce_sum | solution.py:23
  27.8 0.2 multiply_reduce_fusion.2
  28.0 0.0 copy-done.4
  28.0 1.8 convolution_convert_fusion
  29.9 12.0 %all-to-all-start = ((bf16[32,16,1536]{2,1,0:T(8,128)(2,1)}), bf16[32,16,1536]{2,1,0:T(8,128)(2,1)S(1)}, u32[]{:S(2)}, u32[]{:S(2)}) async-start(bf16[32,16,1536]{2,1,0:T(8,128)(2,1)} %bitcast.4), calls=%async_computation | async-start | bytes 3145728 | tf_op jit(solution)/shard_map/all_to_all | solution.py:65
  41.9 0.0 all-gather.8.cloned.1.call-start
  41.9 0.7 all-gather.8.cloned.1.call-update
  42.6 37.3 %all-to-all-done = bf16[32,16,1536]{2,1,0:T(8,128)(2,1)S(1)} async-done(((bf16[32,16,1536]{2,1,0:T(8,128)(2,1)}), bf16[32,16,1536]{2,1,0:T(8,128)(2,1)S(1)}, u32[]{:S(2)}, u32[]{:S(2)}) %all-to-all-start) | async-done | bytes 1572896 | tf_op jit(solution)/shard_map/all_to_all | solution.py:65
  79.9 0.0 all-gather.4.cloned.1.call-done
  79.9 6.2 %multiply_convert_fusion = bf16[512,1536]{1,0:T(8,128)(2,1)} fusion(bf16[512,1536]{1,0:T(8,128)(2,1)S(1)} %bitcast.68, bf16[1,1536,1536]{2,1,0:T(8,128)(2,1)} %all-gather.4.cloned.1.call-done), kind=kOutput, calls=%fused_computation.4 | convolution fusion | flops 2419851264 | bytes 7864320 | tf_op jit(solution)/shard_map/dot_general | solution.py:67
  86.1 15.2 %all-gather.6.cloned.1.call-done = bf16[1,1536,768]{2,1,0:T(8,128)(2,1)} async-done(((bf16[1,96,768]{2,1,0:T(8,128)(2,1)}), bf16[1,1536,768]{2,1,0:T(8,128)(2,1)}) %all-gather.6.cloned.1.call-update) | async-done | bytes 2359312 | tf_op jit(solution)/shard_map/all_gather | solution.py:62
  101.3 4.4 %fusion.8 = bf16[512,768]{1,0:T(8,128)(2,1)} fusion(bf16[512,1536]{1,0:T(8,128)(2,1)} %multiply_convert_fusion, bf16[1,1536,768]{2,1,0:T(8,128)(2,1)} %all-gather.6.cloned.1.call-done), kind=kOutput, calls=%fused_computation.38 | convolution fusion | flops 1208352768 | bytes 4718592 | tf_op jit(solution)/shard_map/dot_general | solution.py:72
  105.7 10.3 %all-to-all-start.1 = ((bf16[32,16,768]{2,1,0:T(8,128)(2,1)}), bf16[32,16,768]{2,1,0:T(8,128)(2,1)S(1)}, u32[]{:S(2)}, u32[]{:S(2)}) async-start(bf16[32,16,768]{2,1,0:T(8,128)(2,1)} %bitcast.8), calls=%async_computation.1 | async-start | bytes 1572864 | tf_op jit(solution)/shard_map/all_to_all | solution.py:75
  116.0 0.0 copy-start.6
  116.0 28.4 %all-gather.8.cloned.1.call-done = bf16[1,1536,768]{2,1,0:T(8,128)(2,1)} async-done(((bf16[1,96,768]{2,1,0:T(8,128)(2,1)}), bf16[1,1536,768]{2,1,0:T(8,128)(2,1)}) %all-gather.8.cloned.1.call-update) | async-done | bytes 2359312 | tf_op jit(solution)/shard_map/all_gather | solution.py:62
  144.4 4.4 %fusion.11 = bf16[512,768]{1,0:T(8,128)(2,1)} fusion(bf16[512,1536]{1,0:T(8,128)(2,1)} %multiply_convert_fusion, bf16[1,1536,768]{2,1,0:T(8,128)(2,1)} %all-gather.8.cloned.1.call-done), kind=kOutput, calls=%fused_computation.39 | convolution fusion | flops 1208352768 | bytes 4718592 | tf_op jit(solution)/shard_map/dot_general | solution.py:72
  148.9 0.0 all-to-all-done.1
  148.9 10.3 %all-to-all-start.2 = ((bf16[32,16,768]{2,1,0:T(8,128)(2,1)}), bf16[32,16,768]{2,1,0:T(8,128)(2,1)S(1)}, u32[]{:S(2)}, u32[]{:S(2)}) async-start(bf16[32,16,768]{2,1,0:T(8,128)(2,1)} %bitcast.11), calls=%async_computation.2 | async-start | bytes 1572864 | tf_op jit(solution)/shard_map/all_to_all | solution.py:75
  159.2 0.0 copy-done.6
  159.2 0.1 copy.26
  159.4 1.2 gather_fusion
  160.5 22.0 %all-to-all-done.2 = bf16[32,16,768]{2,1,0:T(8,128)(2,1)S(1)} async-done(((bf16[32,16,768]{2,1,0:T(8,128)(2,1)}), bf16[32,16,768]{2,1,0:T(8,128)(2,1)S(1)}, u32[]{:S(2)}, u32[]{:S(2)}) %all-to-all-start.2) | async-done | bytes 786464 | tf_op jit(solution)/shard_map/all_to_all | solution.py:75
  182.5 1.2 gather_fusion.1
  183.7 0.2 select_convert_fusion
  183.9 0.5 reshape.84
  184.4 0.5 reshape.85
  184.9 2.1 %multiply_reduce_fusion.1 = (f32[128,768]{1,0:T(8,128)S(1)}, f32[128,768]{1,0:T(8,128)S(1)}) fusion(f32[128,2,768]{2,1,0:T(2,128)S(1)} %reshape.84, f32[128,2]{1,0:T(8,128)S(1)} %copy.26, f32[128,2,768]{2,1,0:T(2,128)S(1)} %reshape.85), kind=kLoop, calls=%fused_computation.53 | loop fusion | flops 589824 | bytes 2360320 | tf_op jit(solution)/shard_map/reduce_sum | solution.py:84
  187.0 0.9 fusion.24
  (11 shorter events, 0.1 us)
Async XLA Ops:
  6.5 16.9 %copy-start = (bf16[1,128,1536]{2,1,0:T(8,128)(2,1)S(1)}, bf16[1,128,1536]{2,1,0:T(8,128)(2,1)}, u32[]{:S(2)}) copy-start(bf16[1,128,1536]{2,1,0:T(8,128)(2,1)} %param.12) | copy-start | bytes 1179652
  6.5 14.5 %copy-start.5 = (s32[1,128,2]{1,2,0:T(2,128)S(1)}, s32[1,128,2]{1,2,0:T(2,128)}, u32[]{:S(2)}) copy-start(s32[1,128,2]{1,2,0:T(2,128)} %param.18) | copy-start | bytes 3076
  6.5 16.0 %copy-start.1 = (f32[31,1536]{1,0:T(8,128)S(1)}, f32[31,1536]{1,0:T(8,128)}, u32[]{:S(2)}) copy-start(f32[31,1536]{1,0:T(8,128)} %param.14) | copy-start | bytes 571396
  6.5 16.9 %copy-start.3 = (f32[1536]{0:T(1024)S(1)}, f32[1536]{0:T(1024)}, u32[]{:S(2)}) copy-start(f32[1536]{0:T(1024)} %param.15) | copy-start | bytes 18436
  6.5 16.9 %copy-start.2 = (f32[1536]{0:T(1024)S(1)}, f32[1536]{0:T(1024)}, u32[]{:S(2)}) copy-start(f32[1536]{0:T(1024)} %param.16) | copy-start | bytes 18436
  6.5 73.4 %all-gather.4.cloned.1.call-start = ((), (), s32[]{:S(2)}) async-start(), calls=%async_computation.3 | async-start | bytes 5013504 | tf_op jit(solution)/shard_map/all_gather | solution.py:60
  7.3 94.0 %all-gather.6.cloned.1.call-start = ((), (), s32[]{:S(2)}) async-start(), calls=%async_computation.4 | async-start | bytes 2506752 | tf_op jit(solution)/shard_map/all_gather | solution.py:62
  11.5 16.6 %copy-start.4 = (f32[1536]{0:T(1024)S(1)}, f32[1536]{0:T(1024)}, u32[]{:S(2)}) copy-start(f32[1536]{0:T(1024)} %param.17) | copy-start | bytes 18436
  12.8 10.4 %collective-permute-start = (bf16[15,1536]{1,0:T(8,128)(2,1)S(1)}, bf16[15,1536]{1,0:T(8,128)(2,1)S(1)}, u32[]{:S(2)}, u32[]{:S(2)}) collective-permute-start(bf16[15,1536]{1,0:T(8,128)(2,1)S(1)} %get-tuple-element.43), channel_id=1, source_target_pairs={{0,1},{1,2},{2,3},{3,4},{4,5},{5,6},{6,7},{7,8},{8,9},{9,10},{10,1... | collective-permute-start | bytes 138248 | tf_op jit(solution)/shard_map/ppermute | solution.py:14
  17.1 6.3 %collective-permute-start.1 = (bf16[15,1536]{1,0:T(8,128)(2,1)S(1)}, bf16[15,1536]{1,0:T(8,128)(2,1)S(1)}, u32[]{:S(2)}, u32[]{:S(2)}) collective-permute-start(bf16[15,1536]{1,0:T(8,128)(2,1)S(1)} %get-tuple-element.44), channel_id=1, source_target_pairs={{1,0},{2,1},{3,2},{4,3},{5,4},{6,5},{7,6},{8,7},{9,8},{10,9},{11,1... | collective-permute-start | bytes 138248 | tf_op jit(solution)/shard_map/ppermute | solution.py:17
  29.9 50.0 %all-to-all-start = ((bf16[32,16,1536]{2,1,0:T(8,128)(2,1)}), bf16[32,16,1536]{2,1,0:T(8,128)(2,1)S(1)}, u32[]{:S(2)}, u32[]{:S(2)}) async-start(bf16[32,16,1536]{2,1,0:T(8,128)(2,1)} %bitcast.4), calls=%async_computation | async-start | bytes 3145728 | tf_op jit(solution)/shard_map/all_to_all | solution.py:65
  41.9 102.6 %all-gather.8.cloned.1.call-start = ((), (), s32[]{:S(2)}) async-start(), calls=%async_computation.5 | async-start | bytes 2506752 | tf_op jit(solution)/shard_map/all_gather | solution.py:62
  105.7 43.1 %all-to-all-start.1 = ((bf16[32,16,768]{2,1,0:T(8,128)(2,1)}), bf16[32,16,768]{2,1,0:T(8,128)(2,1)S(1)}, u32[]{:S(2)}, u32[]{:S(2)}) async-start(bf16[32,16,768]{2,1,0:T(8,128)(2,1)} %bitcast.8), calls=%async_computation.1 | async-start | bytes 1572864 | tf_op jit(solution)/shard_map/all_to_all | solution.py:75
  116.0 43.2 %copy-start.6 = (f32[1,128,2]{1,2,0:T(2,128)S(1)}, f32[1,128,2]{1,2,0:T(2,128)}, u32[]{:S(2)}) copy-start(f32[1,128,2]{1,2,0:T(2,128)} %param.19) | copy-start | bytes 3076
  148.9 33.7 %all-to-all-start.2 = ((bf16[32,16,768]{2,1,0:T(8,128)(2,1)}), bf16[32,16,768]{2,1,0:T(8,128)(2,1)S(1)}, u32[]{:S(2)}, u32[]{:S(2)}) async-start(bf16[32,16,768]{2,1,0:T(8,128)(2,1)} %bitcast.11), calls=%async_computation.2 | async-start | bytes 1572864 | tf_op jit(solution)/shard_map/all_to_all | solution.py:75
Sparse Core Ops, SparseCore 0:
  9.5 48.6 all-gather.3
  60.3 40.9 all-gather.5
  103.5 40.9 all-gather.7

commit v2 on v0

--- a/solution.py
+++ b/solution.py
@@ -55,10 +55,8 @@
     )
     outgoing = jnp.dot(placing.astype(jnp.bfloat16), routed, preferred_element_type=jnp.float32)
     outgoing = outgoing.astype(jnp.bfloat16).reshape(experts_all, capacity, width)
-    full_in, full_out = (
-        lax.all_gather(w_in, "fsdp", axis=1, tiled=True),
-        lax.all_gather(w_out, "fsdp", axis=1, tiled=True),
-    )
+    both = lax.all_gather(jnp.concatenate([w_in, w_out], axis=0), "fsdp", axis=1, tiled=True)
+    full_in, full_out = both[0:1], both[1:2]
     block = lax.all_to_all(outgoing, "expert", split_axis=0, concat_axis=0, tiled=True)
     rows_in = block.reshape(-1, width)
     hidden = jax.nn.silu(jnp.dot(rows_in, full_in[0], preferred_element_type=jnp.float32)).astype(

time: 177 us -> 150 us (0.85)
  the two profiles are of different devices: /device:TPU:8 before, /device:TPU:24 now
where the time goes in v2:
time: 150 us; the launch traced here: 149 us
  blocking collectives  51.2 us (34%)
  waiting for transfers between devices  41.8 us (28%)
  other arithmetic  15 us (10%)
  between operations  13.6 us (9%)
  starting transfers between devices  13.3 us (9%)
  matrix products  10.9 us (7%)
  local copies, waits for them, and re-layouts  3.6 us (2%)
    all_to_all x1, blocking collectives, shards(): lax.all_to_all(outgoing, 'expert', split_axis=0, concat_axis=0, tiled=True)  51.2 us
    all_to_all x1, waiting for transfers between devices, shards(): lax.all_to_all(result.reshape(block.shape), 'expert', split_axis=0, conca...  38.9 us
    dot_general x1, matrix products, shards(): jnp.dot(hidden, full_out[0], preferred_element_type=jnp.float32)  10.3 us
    all_to_all x1, starting transfers between devices, shards(): lax.all_to_all(result.reshape(block.shape), 'expert', split_axis=0, conca...  7.65 us
    reduce_sum x2, other arithmetic, layer_norm(): centre = jnp.mean(values, axis=-1, keepdims=True)  5.48 us
    ppermute x1, starting transfers between devices, padded_2(): lax.ppermute(lax.slice_in_dim(block, block.shape[dim] - width, None, axis...  4.28 us
    reduce_sum x1, other arithmetic, shards(): combined = jnp.sum(gates[0][:, :, None] * picked, axis=1)  3.1 us
  transfers between devices with their start and end apart: 4, of which 2 were waited for; matrix products, arithmetic and copies ran while one was open for 8% of the time, Pallas kernels for 0%

profile of v2, /device:TPU:24, one launch (start us, length us, event | category | flops | bytes accessed | tf_op | source)
XLA Modules:
  0.0 149.4 jit_solution(13750227997531271294)
XLA Ops:
  6.5 0.0 copy-start
  6.5 0.0 copy-start.2
  6.5 0.0 copy-start.1
  6.5 0.0 copy-start.4
  6.5 0.0 copy-start.3
  6.5 0.0 all-gather.2.cloned.1.call-start
  6.6 2.0 %pad_maximum_fusion = bf16[2,96,1536]{2,1,0:T(8,128)(2,1)} fusion(bf16[1,96,1536]{2,1,0:T(8,128)(2,1)} %param.19, bf16[1,96,1536]{2,1,0:T(8,128)(2,1)} %param.18), kind=kLoop, calls=%fused_computation.50 | loop fusion | flops 294912 | bytes 1179648 | tf_op jit(solution)/shard_map/concatenate | solution.py:58
  8.6 0.0 copy-start.5
  8.6 0.0 all-gather.2.cloned.1.call-update
  8.6 1.1 convert_reduce_fusion
  9.7 1.2 fusion.7
  11.0 1.3 fusion.9
  12.3 4.3 %collective-permute-start = (bf16[15,1536]{1,0:T(8,128)(2,1)S(1)}, bf16[15,1536]{1,0:T(8,128)(2,1)S(1)}, u32[]{:S(2)}, u32[]{:S(2)}) collective-permute-start(bf16[15,1536]{1,0:T(8,128)(2,1)S(1)} %get-tuple-element.38), channel_id=1, source_target_pairs={{0,1},{1,2},{2,3},{3,4},{4,5},{5,6},{6,7},{7,8},{8,9},{9,10},{10,1... | collective-permute-start | bytes 138248 | tf_op jit(solution)/shard_map/ppermute | solution.py:14
  16.6 1.3 collective-permute-start.1
  17.9 0.0 copy-done.2
  17.9 0.1 copy.26
  18.0 0.1 eq.41
  18.2 0.1 reshape_squeeze.3
  18.3 0.6 reduce-window.6
  18.9 0.2 slice_reduce_fusion
  19.1 0.1 fusion.45
  19.2 0.1 reduce_sum.64
  19.4 0.1 copy.31
  19.5 0.0 copy-done.1
  19.5 0.2 slice_reduce_fusion.30
  19.7 0.3 slice_reduce_fusion.31
  20.0 0.1 fusion.10
  20.1 0.0 collective-permute-done
  20.1 2.9 %collective-permute-done.1 = bf16[15,1536]{1,0:T(8,128)(2,1)S(1)} collective-permute-done((bf16[15,1536]{1,0:T(8,128)(2,1)S(1)}, bf16[15,1536]{1,0:T(8,128)(2,1)S(1)}, u32[]{:S(2)}, u32[]{:S(2)}) %collective-permute-start.1) | collective-permute-done | bytes 46112 | tf_op jit(solution)/shard_map/ppermute | solution.py:17
  22.9 0.0 copy-done
  22.9 0.0 copy-done.4
  22.9 0.0 copy-done.3
  23.0 4.3 %fusion.48 = (f32[128]{0:T(128)S(1)}, f32[128,1536]{1,0:T(8,128)S(1)}) fusion(f32[1536]{0:T(1024)S(1)} %copy-done.3, bf16[15,1536]{1,0:T(8,128)(2,1)S(1)} %collective-permute-done.1, bf16[128,1536]{1,0:T(8,128)(2,1)S(1)} %fusion.9, f32[1536]{0:T(1024)S(1)} %get-tuple-element.34, f32[1536]{0:T(1024)S(1)} %get-tuple-element.35, ...), kind=kLoop, calls=%fused_computation.159 | loop fusion | flops 37552000 | bytes 1868288 | tf_op jit(solution)/shard_map/reduce_sum | solution.py:23
  27.3 0.2 multiply_reduce_fusion.1
  27.6 0.0 copy-done.5
  27.6 0.7 convolution_convert_fusion
  28.2 51.2 %all_to_all.10 = bf16[32,16,1536]{2,1,0:T(8,128)(2,1)S(1)} all-to-all(bf16[32,16,1536]{2,1,0:T(8,128)(2,1)S(1)} %bitcast.66), channel_id=1, replica_groups=mesh['fsdp'=16,'expert'=32] {'expert'}, dimensions={0} | all-to-all | bytes 3145728 | tf_op jit(solution)/shard_map/all_to_all | solution.py:60
  79.4 0.0 all-gather.2.cloned.1.call-done
  79.5 10.3 %fusion.2 = bf16[512,1536]{1,0:T(8,128)(2,1)} fusion(bf16[2,1536,1536]{2,1,0:T(8,128)(2,1)} %all-gather.2.cloned.1.call-done, bf16[512,1536]{1,0:T(8,128)(2,1)S(1)} %bitcast.68), kind=kOutput, calls=%fused_computation.6 | convolution fusion | flops 4836556800 | bytes 12582912 | tf_op jit(solution)/shard_map/dot_general | solution.py:65
  89.7 0.0 copy-start.6
  89.7 7.7 %all-to-all-start.1 = ((bf16[32,16,1536]{2,1,0:T(8,128)(2,1)}), bf16[32,16,1536]{2,1,0:T(8,128)(2,1)S(1)}, u32[]{:S(2)}, u32[]{:S(2)}) async-start(bf16[32,16,1536]{2,1,0:T(8,128)(2,1)} %bitcast.67), calls=%async_computation.1 | async-start | bytes 3145728 | tf_op jit(solution)/shard_map/all_to_all | solution.py:66
  97.4 0.1 reduce_sum.63
  97.5 0.1 copy.32
  97.6 0.1 mul.519
  97.8 0.1 copy.29
  97.9 0.1 copy.30
  98.0 0.0 copy-done.6
  98.0 0.1 copy.25
  98.2 38.9 %all-to-all-done.1 = bf16[32,16,1536]{2,1,0:T(8,128)(2,1)S(1)} async-done(((bf16[32,16,1536]{2,1,0:T(8,128)(2,1)}), bf16[32,16,1536]{2,1,0:T(8,128)(2,1)S(1)}, u32[]{:S(2)}, u32[]{:S(2)}) %all-to-all-start.1) | async-done | bytes 1572896 | tf_op jit(solution)/shard_map/all_to_all | solution.py:66
  137.0 1.3 gather_fusion
  138.3 0.3 gather.7
  138.6 3.1 %multiply_reduce_fusion = f32[128,1536]{1,0:T(8,128)S(1)} fusion(bf16[128,2,1536]{2,1,0:T(2,128)(2,1)S(1)} %gather.7, pred[128,2]{1,0:T(8,128)(4,1)S(1)} %copy.30, f32[128,2]{1,0:T(8,128)S(1)} %copy.25), kind=kLoop, calls=%fused_computation.36 | loop fusion | flops 1376256 | bytes 1574144 | tf_op jit(solution)/shard_map/reduce_sum | solution.py:75
  141.7 0.8 fusion.11
  (12 shorter events, 0.1 us)
Async XLA Ops:
  6.5 16.4 %copy-start = (bf16[1,128,1536]{2,1,0:T(8,128)(2,1)S(1)}, bf16[1,128,1536]{2,1,0:T(8,128)(2,1)}, u32[]{:S(2)}) copy-start(bf16[1,128,1536]{2,1,0:T(8,128)(2,1)} %param.10) | copy-start | bytes 1179652
  6.5 11.4 %copy-start.2 = (s32[1,128,2]{1,2,0:T(2,128)S(1)}, s32[1,128,2]{1,2,0:T(2,128)}, u32[]{:S(2)}) copy-start(s32[1,128,2]{1,2,0:T(2,128)} %param.16) | copy-start | bytes 3076
  6.5 12.9 %copy-start.1 = (f32[31,1536]{1,0:T(8,128)S(1)}, f32[31,1536]{1,0:T(8,128)}, u32[]{:S(2)}) copy-start(f32[31,1536]{1,0:T(8,128)} %param.12) | copy-start | bytes 571396
  6.5 16.4 %copy-start.4 = (f32[1536]{0:T(1024)S(1)}, f32[1536]{0:T(1024)}, u32[]{:S(2)}) copy-start(f32[1536]{0:T(1024)} %param.13) | copy-start | bytes 18436
  6.5 16.4 %copy-start.3 = (f32[1536]{0:T(1024)S(1)}, f32[1536]{0:T(1024)}, u32[]{:S(2)}) copy-start(f32[1536]{0:T(1024)} %param.14) | copy-start | bytes 18436
  6.5 72.9 %all-gather.2.cloned.1.call-start = ((), (), s32[]{:S(2)}) async-start(), calls=%async_computation.2 | async-start | bytes 10027008 | tf_op jit(solution)/shard_map/all_gather | solution.py:58
  8.6 19.0 %copy-start.5 = (f32[1536]{0:T(1024)S(1)}, f32[1536]{0:T(1024)}, u32[]{:S(2)}) copy-start(f32[1536]{0:T(1024)} %param.15) | copy-start | bytes 18436
  12.3 7.8 %collective-permute-start = (bf16[15,1536]{1,0:T(8,128)(2,1)S(1)}, bf16[15,1536]{1,0:T(8,128)(2,1)S(1)}, u32[]{:S(2)}, u32[]{:S(2)}) collective-permute-start(bf16[15,1536]{1,0:T(8,128)(2,1)S(1)} %get-tuple-element.38), channel_id=1, source_target_pairs={{0,1},{1,2},{2,3},{3,4},{4,5},{5,6},{6,7},{7,8},{8,9},{9,10},{10,1... | collective-permute-start | bytes 138248 | tf_op jit(solution)/shard_map/ppermute | solution.py:14
  16.6 6.3 %collective-permute-start.1 = (bf16[15,1536]{1,0:T(8,128)(2,1)S(1)}, bf16[15,1536]{1,0:T(8,128)(2,1)S(1)}, u32[]{:S(2)}, u32[]{:S(2)}) collective-permute-start(bf16[15,1536]{1,0:T(8,128)(2,1)S(1)} %get-tuple-element.39), channel_id=1, source_target_pairs={{1,0},{2,1},{3,2},{4,3},{5,4},{6,5},{7,6},{8,7},{9,8},{10,9},{11,1... | collective-permute-start | bytes 138248 | tf_op jit(solution)/shard_map/ppermute | solution.py:17
  89.7 8.3 %copy-start.6 = (f32[1,128,2]{1,2,0:T(2,128)S(1)}, f32[1,128,2]{1,2,0:T(2,128)}, u32[]{:S(2)}) copy-start(f32[1,128,2]{1,2,0:T(2,128)} %param.17) | copy-start | bytes 3076
  89.7 47.3 %all-to-all-start.1 = ((bf16[32,16,1536]{2,1,0:T(8,128)(2,1)}), bf16[32,16,1536]{2,1,0:T(8,128)(2,1)S(1)}, u32[]{:S(2)}, u32[]{:S(2)}) async-start(bf16[32,16,1536]{2,1,0:T(8,128)(2,1)} %bitcast.67), calls=%async_computation.1 | async-start | bytes 3145728 | tf_op jit(solution)/shard_map/all_to_all | solution.py:66
Sparse Core Ops, SparseCore 0:
  9.5 67.2 all-gather.1

commit v3 on v2

--- a/solution.py
+++ b/solution.py
@@ -35,28 +35,32 @@
     experts_all = lax.axis_size("expert") * w_in.shape[0]
     capacity = 2 * picks_per * frame_count // experts_all
     slots_all = experts_all * capacity
+    both = lax.all_gather(jnp.concatenate([w_in, w_out], axis=0), "fsdp", axis=1, tiled=True)
+    full_in, full_out = both[0:1], both[1:2]
+    raw = padded_2(frames[0], (("expert", 0),), reach)
+    padded = layer_norm(raw.astype(jnp.float32), ln_gain).astype(jnp.bfloat16)
     stream = frames[0].astype(jnp.float32)
-    normed = layer_norm(stream, ln_gain).astype(jnp.bfloat16)
-    padded = padded_2(normed, (("expert", 0),), reach)
     filtered = jnp.zeros(stream.shape, jnp.float32)
     for offset in range(taps):
         filtered = filtered + kernel[offset] * padded[offset : offset + frame_count]
     mixed = stream + jax.nn.silu(bn_scale * filtered + bn_shift)
     routed = layer_norm(mixed, ffn_gain).astype(jnp.bfloat16)
     chosen = expert_ids[0].reshape(-1)
+    picks = chosen.shape[0]
     onehot = (chosen[:, None] == jnp.arange(experts_all, dtype=jnp.int32)[None, :]).astype(
-        jnp.int32
+        jnp.bfloat16
     )
-    before = jnp.cumsum(onehot, axis=0) - onehot
-    slot_at = jnp.sum(before * onehot, axis=1)
+    lower = (
+        jnp.arange(picks, dtype=jnp.int32)[:, None] > jnp.arange(picks, dtype=jnp.int32)[None, :]
+    ).astype(jnp.bfloat16)
+    before = jnp.dot(lower, onehot, preferred_element_type=jnp.float32)
+    slot_at = jnp.sum(before * onehot.astype(jnp.float32), axis=1).astype(jnp.int32)
     target = (chosen * capacity + slot_at).reshape(frame_count, picks_per)
     placing = jnp.any(
         target[None, :, :] == jnp.arange(slots_all, dtype=jnp.int32)[:, None, None], axis=2
     )
     outgoing = jnp.dot(placing.astype(jnp.bfloat16), routed, preferred_element_type=jnp.float32)
     outgoing = outgoing.astype(jnp.bfloat16).reshape(experts_all, capacity, width)
-    both = lax.all_gather(jnp.concatenate([w_in, w_out], axis=0), "fsdp", axis=1, tiled=True)
-    full_in, full_out = both[0:1], both[1:2]
     block = lax.all_to_all(outgoing, "expert", split_axis=0, concat_axis=0, tiled=True)
     rows_in = block.reshape(-1, width)
     hidden = jax.nn.silu(jnp.dot(rows_in, full_in[0], preferred_element_type=jnp.float32)).astype(
@@ -67,12 +71,15 @@
         result.reshape(block.shape), "expert", split_axis=0, concat_axis=0, tiled=True
     )
     rows_back = returned.reshape(-1, width)
-    picked = (
-        jnp.take(rows_back, target.reshape(-1), axis=0)
-        .reshape(frame_count, picks_per, width)
-        .astype(jnp.float32)
+    select = (
+        target.reshape(-1)[:, None] == jnp.arange(slots_all, dtype=jnp.int32)[None, :]
+    ).astype(jnp.bfloat16)
+    picked = jnp.dot(select, rows_back, preferred_element_type=jnp.float32).reshape(
+        frame_count, picks_per, width
     )
-    combined = jnp.sum(gates[0][:, :, None] * picked, axis=1)
+    combined = gates[0][:, 0][:, None] * picked[:, 0]
+    for k in range(1, picks_per):
+        combined = combined + gates[0][:, k][:, None] * picked[:, k]
     return (mixed + 0.5 * combined).astype(jnp.bfloat16)[None]
 
 

time: 150 us -> 146 us (0.973)
  other arithmetic: 15 us -> 8.01 us
  blocking collectives: 51.2 us -> 53.6 us
  waiting for transfers between devices: 41.8 us -> 39.8 us
  local copies, waits for them, and re-layouts: 3.6 us -> 5.43 us
    reduce_sum x2 -> x0, other arithmetic: 3.2 us -> none  [the longest x1 3.1 us: shards(): combined = jnp.sum(gates[0][:, :, None] * picked, axis=1)]
    slice x2, local copies, waits for them, and re-layouts: 0.53 us -> 3.25 us  [shards(): filtered = filtered + kernel[offset] * padded[offset:offset + frame_count]]
    ppermute x1, waiting for transfers between devices: 2.86 us -> 0.34 us  [padded_2(): lax.ppermute(lax.slice_in_dim(block, 0, width, axis=dim), axis, backward)]
    all_to_all x1, blocking collectives: 51.2 us -> 53.6 us  [shards(): lax.all_to_all(outgoing, 'expert', split_axis=0, concat_axis=0, tiled=True)]
    gather x2 -> x0, local copies, waits for them, and re-layouts: 1.56 us -> none  [shards(): jnp.take(rows_back, target.reshape(-1), axis=0)]
    reduce_sum x2, other arithmetic: 5.48 us -> 3.96 us  [layer_norm(): centre = jnp.mean(values, axis=-1, keepdims=True)]
where the time goes in v3:
time: 146 us
  blocking collectives  53.6 us (37%)
  waiting for transfers between devices  39.8 us (27%)
  between operations  13.6 us (9%)
  starting transfers between devices  13.3 us (9%)
  matrix products  11.8 us (8%)
  other arithmetic  8.01 us (5%)
  local copies, waits for them, and re-layouts  5.43 us (4%)
    all_to_all x1, blocking collectives, shards(): lax.all_to_all(outgoing, 'expert', split_axis=0, concat_axis=0, tiled=True)  53.6 us
    all_to_all x1, waiting for transfers between devices, shards(): lax.all_to_all(result.reshape(block.shape), 'expert', split_axis=0, conca...  39.4 us
    dot_general x1, matrix products, shards(): jnp.dot(hidden, full_out[0], preferred_element_type=jnp.float32)  10.3 us
    all_to_all x1, starting transfers between devices, shards(): lax.all_to_all(result.reshape(block.shape), 'expert', split_axis=0, conca...  7.68 us
    ppermute x1, starting transfers between devices, padded_2(): lax.ppermute(lax.slice_in_dim(block, block.shape[dim] - width, None, axis...  4.28 us
    reduce_sum x2, other arithmetic, layer_norm(): centre = jnp.mean(values, axis=-1, keepdims=True)  3.96 us
    slice x2, local copies, waits for them, and re-layouts, shards(): filtered = filtered + kernel[offset] * padded[offset:offset + frame_count]  3.25 us
  transfers between devices with their start and end apart: 4, of which 2 were waited for; matrix products, arithmetic and copies ran while one was open for 8% of the time, Pallas kernels for 0%

profile of v3, /device:TPU:24, one launch (start us, length us, event | category | flops | bytes accessed | tf_op | source)
XLA Modules:
  0.0 145.5 jit_solution(18287025929815170760)
XLA Ops:
  6.5 0.0 copy-start
  6.5 0.0 copy-start.1
  6.5 0.0 copy-start.2
  6.5 0.0 copy-start.3
  6.5 0.0 all-gather.2.cloned.1.call-start
  6.6 2.0 %pad_maximum_fusion = bf16[2,96,1536]{2,1,0:T(8,128)(2,1)} fusion(bf16[1,96,1536]{2,1,0:T(8,128)(2,1)} %param.19, bf16[1,96,1536]{2,1,0:T(8,128)(2,1)} %param.18), kind=kLoop, calls=%fused_computation.27 | loop fusion | flops 294912 | bytes 1179648 | tf_op jit(solution)/shard_map/concatenate | solution.py:38
  8.5 0.0 all-gather.2.cloned.1.call-update
  8.6 0.8 slice_bitcast_fusion.13
  9.4 4.3 %collective-permute-start = (bf16[15,1536]{1,0:T(8,128)(2,1)S(1)}, bf16[15,1536]{1,0:T(8,128)(2,1)S(1)}, u32[]{:S(2)}, u32[]{:S(2)}) collective-permute-start(bf16[15,1536]{1,0:T(8,128)(2,1)S(1)} %get-tuple-element.38), channel_id=1, source_target_pairs={{0,1},{1,2},{2,3},{3,4},{4,5},{5,6},{6,7},{7,8},{8,9},{9,10},{10,1... | collective-permute-start | bytes 138248 | tf_op jit(solution)/shard_map/ppermute | solution.py:14
  13.7 1.3 collective-permute-start.1
  15.0 0.8 copy.15
  15.8 0.1 eq.59
  15.9 0.2 fusion.5
  16.1 0.1 convert_element_type.184
  16.3 0.1 copy.18
  16.4 1.5 %slice_reduce_fusion.29 = (f32[1536]{0:T(1024)S(1)}, f32[1536]{0:T(1024)S(1)}, f32[1536]{0:T(1024)S(1)}, f32[1536]{0:T(1024)S(1)}, f32[1536]{0:T(1024)S(1)}, /*i...) fusion(f32[31,1536]{1,0:T(8,128)} %param.12), kind=kLoop, calls=%fused_computation.76 | loop fusion | bytes 147456 | tf_op jit(solution)/shard_map/slice | solution.py:45
  17.8 1.8 %slice_reduce_fusion.30 = (f32[1536]{0:T(1024)S(1)}, f32[1536]{0:T(1024)S(1)}, f32[1536]{0:T(1024)S(1)}, f32[1536]{0:T(1024)S(1)}, f32[1536]{0:T(1024)S(1)}, /*i...) fusion(f32[31,1536]{1,0:T(8,128)} %param.12), kind=kLoop, calls=%fused_computation.77 | loop fusion | bytes 233472 | tf_op jit(solution)/shard_map/slice | solution.py:45
  19.6 0.1 fusion.18
  19.7 0.0 collective-permute-done
  19.7 0.3 collective-permute-done.1
  20.0 0.0 copy-done
  20.0 0.2 convert_reduce_fusion
  20.3 0.3 fusion.6
  20.6 0.0 copy-done.1
  20.6 0.4 fusion.8
  21.1 0.0 copy-done.2
  21.1 0.0 copy-done.3
  21.1 0.0 copy-start.4
  21.1 3.7 %fusion.27 = (f32[128]{0:T(128)S(1)}, f32[128,1536]{1,0:T(8,128)S(1)}) fusion(f32[1536]{0:T(1024)S(1)} %copy-done.2, bf16[158,1536]{1,0:T(8,128)(2,1)S(1)} %fusion.8, f32[1536]{0:T(1024)S(1)} %get-tuple-element.34, f32[1536]{0:T(1024)S(1)} %get-tuple-element.35, f32[1536]{0:T(1024)S(1)} %get-tuple-element.6, f32[1536]{0:T(1024)S(1)} %get-tuple-element.7, ...), kind=kLoop, calls=%fused_computation.85 | loop fusion | flops 19857280 | bytes 13572608 | tf_op jit(solution)/shard_map/reduce_sum | solution.py:23
  24.9 0.2 multiply_reduce_fusion
  25.1 0.0 copy-done.4
  25.1 0.7 convolution_convert_fusion
  25.8 53.6 %all_to_all.10 = bf16[32,16,1536]{2,1,0:T(8,128)(2,1)S(1)} all-to-all(bf16[32,16,1536]{2,1,0:T(8,128)(2,1)S(1)} %bitcast.68), channel_id=1, replica_groups=mesh['fsdp'=16,'expert'=32] {'expert'}, dimensions={0} | all-to-all | bytes 3145728 | tf_op jit(solution)/shard_map/all_to_all | solution.py:64
  79.4 0.0 all-gather.2.cloned.1.call-done
  79.4 10.3 %fusion.2 = bf16[512,1536]{1,0:T(8,128)(2,1)} fusion(bf16[2,1536,1536]{2,1,0:T(8,128)(2,1)} %all-gather.2.cloned.1.call-done, bf16[512,1536]{1,0:T(8,128)(2,1)S(1)} %bitcast.70), kind=kOutput, calls=%fused_computation.5 | convolution fusion | flops 4836556800 | bytes 12582912 | tf_op jit(solution)/shard_map/dot_general | solution.py:69
  89.7 0.0 copy-start.5
  89.7 7.7 %all-to-all-start.1 = ((bf16[32,16,1536]{2,1,0:T(8,128)(2,1)}), bf16[32,16,1536]{2,1,0:T(8,128)(2,1)S(1)}, u32[]{:S(2)}, u32[]{:S(2)}) async-start(bf16[32,16,1536]{2,1,0:T(8,128)(2,1)} %bitcast.69), calls=%async_computation.1 | async-start | bytes 3145728 | tf_op jit(solution)/shard_map/all_to_all | solution.py:70
  97.4 0.1 convert_element_type.183
  97.6 0.1 copy.17
  97.6 0.0 copy-done.5
  97.7 39.4 %all-to-all-done.1 = bf16[32,16,1536]{2,1,0:T(8,128)(2,1)S(1)} async-done(((bf16[32,16,1536]{2,1,0:T(8,128)(2,1)}), bf16[32,16,1536]{2,1,0:T(8,128)(2,1)S(1)}, u32[]{:S(2)}, u32[]{:S(2)}) %all-to-all-start.1) | async-done | bytes 1572896 | tf_op jit(solution)/shard_map/all_to_all | solution.py:70
  137.1 0.6 fusion.16
  137.7 1.0 fusion.19
  (8 shorter events, 0.1 us)
Async XLA Ops:
  6.5 13.5 %copy-start = (bf16[1,128,1536]{2,1,0:T(8,128)(2,1)S(1)}, bf16[1,128,1536]{2,1,0:T(8,128)(2,1)}, u32[]{:S(2)}) copy-start(bf16[1,128,1536]{2,1,0:T(8,128)(2,1)} %param.10) | copy-start | bytes 1179652
  6.5 14.1 %copy-start.1 = (f32[1536]{0:T(1024)S(1)}, f32[1536]{0:T(1024)}, u32[]{:S(2)}) copy-start(f32[1536]{0:T(1024)} %param.11) | copy-start | bytes 18436
  6.5 14.5 %copy-start.2 = (f32[1536]{0:T(1024)S(1)}, f32[1536]{0:T(1024)}, u32[]{:S(2)}) copy-start(f32[1536]{0:T(1024)} %param.14) | copy-start | bytes 18436
  6.5 14.5 %copy-start.3 = (f32[1536]{0:T(1024)S(1)}, f32[1536]{0:T(1024)}, u32[]{:S(2)}) copy-start(f32[1536]{0:T(1024)} %param.13) | copy-start | bytes 18436
  6.5 72.9 %all-gather.2.cloned.1.call-start = ((), (), s32[]{:S(2)}) async-start(), calls=%async_computation.2 | async-start | bytes 10027008 | tf_op jit(solution)/shard_map/all_gather | solution.py:38
  9.4 10.3 %collective-permute-start = (bf16[15,1536]{1,0:T(8,128)(2,1)S(1)}, bf16[15,1536]{1,0:T(8,128)(2,1)S(1)}, u32[]{:S(2)}, u32[]{:S(2)}) collective-permute-start(bf16[15,1536]{1,0:T(8,128)(2,1)S(1)} %get-tuple-element.38), channel_id=1, source_target_pairs={{0,1},{1,2},{2,3},{3,4},{4,5},{5,6},{6,7},{7,8},{8,9},{9,10},{10,1... | collective-permute-start | bytes 138248 | tf_op jit(solution)/shard_map/ppermute | solution.py:14
  13.7 6.3 %collective-permute-start.1 = (bf16[15,1536]{1,0:T(8,128)(2,1)S(1)}, bf16[15,1536]{1,0:T(8,128)(2,1)S(1)}, u32[]{:S(2)}, u32[]{:S(2)}) collective-permute-start(bf16[15,1536]{1,0:T(8,128)(2,1)S(1)} %get-tuple-element.39), channel_id=1, source_target_pairs={{1,0},{2,1},{3,2},{4,3},{5,4},{6,5},{7,6},{8,7},{9,8},{10,9},{11,1... | collective-permute-start | bytes 138248 | tf_op jit(solution)/shard_map/ppermute | solution.py:17
  21.1 4.0 %copy-start.4 = (f32[1536]{0:T(1024)S(1)}, f32[1536]{0:T(1024)}, u32[]{:S(2)}) copy-start(f32[1536]{0:T(1024)} %param.15) | copy-start | bytes 18436
  89.7 7.9 %copy-start.5 = (f32[1,128,2]{1,2,0:T(2,128)S(1)}, f32[1,128,2]{1,2,0:T(2,128)}, u32[]{:S(2)}) copy-start(f32[1,128,2]{1,2,0:T(2,128)} %param.17) | copy-start | bytes 3076
  89.7 47.3 %all-to-all-start.1 = ((bf16[32,16,1536]{2,1,0:T(8,128)(2,1)}), bf16[32,16,1536]{2,1,0:T(8,128)(2,1)S(1)}, u32[]{:S(2)}, u32[]{:S(2)}) async-start(bf16[32,16,1536]{2,1,0:T(8,128)(2,1)} %bitcast.69), calls=%async_computation.1 | async-start | bytes 3145728 | tf_op jit(solution)/shard_map/all_to_all | solution.py:70
Sparse Core Ops, SparseCore 0:
  9.5 67.2 all-gather.1

commit v4 on v3

--- a/solution.py
+++ b/solution.py
@@ -1,6 +1,8 @@
 import jax
 import jax.numpy as jnp
 from jax import lax
+from jax.experimental import pallas as pl
+from jax.experimental.pallas import tpu as pltpu
 from jax.sharding import PartitionSpec as P
 
 eps_norm = 1e-05
@@ -19,6 +21,26 @@
     return block
 
 
+def stack_pair(first, second):
+    def body(first_ref, second_ref, out_ref, sems):
+        copies = (
+            pltpu.make_async_copy(first_ref, out_ref.at[0:1], sems.at[0]),
+            pltpu.make_async_copy(second_ref, out_ref.at[1:2], sems.at[1]),
+        )
+        for copy in copies:
+            copy.start()
+        for copy in copies:
+            copy.wait()
+
+    return pl.pallas_call(
+        body,
+        out_shape=jax.ShapeDtypeStruct((2,) + first.shape[1:], first.dtype),
+        in_specs=[pl.BlockSpec(memory_space=pl.ANY), pl.BlockSpec(memory_space=pl.ANY)],
+        out_specs=pl.BlockSpec(memory_space=pl.ANY),
+        scratch_shapes=[pltpu.SemaphoreType.DMA((2,))],
+    )(first, second)
+
+
 def layer_norm(values, gain):
     centre = jnp.mean(values, axis=-1, keepdims=True)
     centred = values - centre
@@ -35,7 +57,7 @@
     experts_all = lax.axis_size("expert") * w_in.shape[0]
     capacity = 2 * picks_per * frame_count // experts_all
     slots_all = experts_all * capacity
-    both = lax.all_gather(jnp.concatenate([w_in, w_out], axis=0), "fsdp", axis=1, tiled=True)
+    both = lax.all_gather(stack_pair(w_in, w_out), "fsdp", axis=1, tiled=True)
     full_in, full_out = both[0:1], both[1:2]
     raw = padded_2(frames[0], (("expert", 0),), reach)
     padded = layer_norm(raw.astype(jnp.float32), ln_gain).astype(jnp.bfloat16)

time: 146 us -> 162 us (1.11)
  Pallas kernels: 0 us -> 19 us
  other arithmetic: 8.01 us -> 6.06 us
    pallas_call x0 -> x1, Pallas kernels: none -> 19 us  [stack_pair(): pl.pallas_call(body, out_shape=jax.ShapeDtypeStruct((2,) + first.shape[1:...]
    concatenate x1 -> x0, other arithmetic: 1.95 us -> none  [shards(): jnp.concatenate([w_in, w_out], axis=0)]
  transfers between devices with their start and end apart: 4 -> 4, of which waited for: 2 -> 2; matrix products, arithmetic and copies ran while one was open for 8% -> 7% of each run, Pallas kernels for 0% -> 0%
where the time goes in v4:
time: 162 us
  blocking collectives  53.6 us (33%)
  waiting for transfers between devices  39.8 us (25%)
  Pallas kernels  19 us (12%)
  between operations  13.6 us (8%)
  starting transfers between devices  12.5 us (8%)
  matrix products  11.8 us (7%)
  other arithmetic  6.06 us (4%)
  local copies, waits for them, and re-layouts  5.43 us (3%)
    all_to_all x1, blocking collectives, shards(): lax.all_to_all(outgoing, 'expert', split_axis=0, concat_axis=0, tiled=True)  53.6 us
    all_to_all x1, waiting for transfers between devices, shards(): lax.all_to_all(result.reshape(block.shape), 'expert', split_axis=0, conca...  39.4 us
    pallas_call x1, Pallas kernels, stack_pair(): pl.pallas_call(body, out_shape=jax.ShapeDtypeStruct((2,) + first.shape[1:...  19 us
    dot_general x1, matrix products, shards(): jnp.dot(hidden, full_out[0], preferred_element_type=jnp.float32)  10.3 us
    all_to_all x1, starting transfers between devices, shards(): lax.all_to_all(result.reshape(block.shape), 'expert', split_axis=0, conca...  6.87 us
    ppermute x1, starting transfers between devices, padded_2(): lax.ppermute(lax.slice_in_dim(block, block.shape[dim] - width, None, axis...  4.28 us
    reduce_sum x2, other arithmetic, layer_norm(): centre = jnp.mean(values, axis=-1, keepdims=True)  3.96 us
    slice x2, local copies, waits for them, and re-layouts, shards(): filtered = filtered + kernel[offset] * padded[offset:offset + frame_count]  3.25 us
  transfers between devices with their start and end apart: 4, of which 2 were waited for; matrix products, arithmetic and copies ran while one was open for 7% of the time, Pallas kernels for 0%

profile of v4, /device:TPU:24, one launch (start us, length us, event | category | flops | bytes accessed | tf_op | source)
XLA Modules:
  0.0 161.8 jit_solution(6596863092510918508)
XLA Ops:
  6.5 0.0 copy-start
  6.5 0.0 copy-start.1
  6.5 0.0 copy-start.2
  6.5 0.0 copy-start.3
  6.5 0.0 all-gather.2.cloned.1.call-start
  6.6 19.0 %shard_map.100 = bf16[2,96,1536]{2,1,0:T(8,128)(2,1)} custom-call(bf16[1,96,1536]{2,1,0:T(8,128)(2,1)} %first_ref.1, bf16[1,96,1536]{2,1,0:T(8,128)(2,1)} %second_ref.1), custom_call_target="tpu_custom_call" | custom-call | tf_op jit(solution)/shard_map/pallas_call | solution.py:35
  25.6 0.0 all-gather.2.cloned.1.call-update
  25.6 0.8 slice_bitcast_fusion.13
  26.4 4.3 %collective-permute-start = (bf16[15,1536]{1,0:T(8,128)(2,1)S(1)}, bf16[15,1536]{1,0:T(8,128)(2,1)S(1)}, u32[]{:S(2)}, u32[]{:S(2)}) collective-permute-start(bf16[15,1536]{1,0:T(8,128)(2,1)S(1)} %get-tuple-element.38), channel_id=1, source_target_pairs={{0,1},{1,2},{2,3},{3,4},{4,5},{5,6},{6,7},{7,8},{8,9},{9,10},{10,1... | collective-permute-start | bytes 138248 | tf_op jit(solution)/shard_map/ppermute | solution.py:16
  30.7 1.3 collective-permute-start.1
  32.0 0.8 copy.15
  32.8 0.1 eq.59
  33.0 0.2 fusion.5
  33.2 0.1 convert_element_type.184
  33.3 0.1 copy.18
  33.4 1.5 slice_reduce_fusion.29
  34.9 1.8 %slice_reduce_fusion.30 = (f32[1536]{0:T(1024)S(1)}, f32[1536]{0:T(1024)S(1)}, f32[1536]{0:T(1024)S(1)}, f32[1536]{0:T(1024)S(1)}, f32[1536]{0:T(1024)S(1)}, /*i...) fusion(f32[31,1536]{1,0:T(8,128)} %param.12), kind=kLoop, calls=%fused_computation.76 | loop fusion | bytes 233472 | tf_op jit(solution)/shard_map/slice | solution.py:67
  36.7 0.1 fusion.18
  36.7 0.0 collective-permute-done
  36.7 0.3 collective-permute-done.1
  37.1 0.0 copy-done
  37.1 0.2 convert_reduce_fusion
  37.3 0.3 fusion.6
  37.7 0.0 copy-done.1
  37.7 0.4 fusion.8
  38.1 0.0 copy-done.2
  38.1 0.0 copy-done.3
  38.1 0.0 copy-start.4
  38.1 3.7 %fusion.27 = (f32[128]{0:T(128)S(1)}, f32[128,1536]{1,0:T(8,128)S(1)}) fusion(f32[1536]{0:T(1024)S(1)} %copy-done.2, bf16[158,1536]{1,0:T(8,128)(2,1)S(1)} %fusion.8, f32[1536]{0:T(1024)S(1)} %get-tuple-element.34, f32[1536]{0:T(1024)S(1)} %get-tuple-element.35, f32[1536]{0:T(1024)S(1)} %get-tuple-element.6, f32[1536]{0:T(1024)S(1)} %get-tuple-element.7, ...), kind=kLoop, calls=%fused_computation.84 | loop fusion | flops 19857280 | bytes 13572608 | tf_op jit(solution)/shard_map/reduce_sum | solution.py:45
  41.9 0.2 multiply_reduce_fusion
  42.1 0.0 copy-done.4
  42.1 0.7 convolution_convert_fusion
  42.8 53.6 %all_to_all.10 = bf16[32,16,1536]{2,1,0:T(8,128)(2,1)S(1)} all-to-all(bf16[32,16,1536]{2,1,0:T(8,128)(2,1)S(1)} %bitcast.68), channel_id=1, replica_groups=mesh['fsdp'=16,'expert'=32] {'expert'}, dimensions={0} | all-to-all | bytes 3145728 | tf_op jit(solution)/shard_map/all_to_all | solution.py:86
  96.5 0.0 all-gather.2.cloned.1.call-done
  96.5 10.3 %fusion.2 = bf16[512,1536]{1,0:T(8,128)(2,1)} fusion(bf16[2,1536,1536]{2,1,0:T(8,128)(2,1)} %all-gather.2.cloned.1.call-done, bf16[512,1536]{1,0:T(8,128)(2,1)S(1)} %bitcast.70), kind=kOutput, calls=%fused_computation.5 | convolution fusion | flops 4836556800 | bytes 12582912 | tf_op jit(solution)/shard_map/dot_general | solution.py:91
  106.8 0.0 copy-start.5
  106.8 6.9 %all-to-all-start.1 = ((bf16[32,16,1536]{2,1,0:T(8,128)(2,1)}), bf16[32,16,1536]{2,1,0:T(8,128)(2,1)S(1)}, u32[]{:S(2)}, u32[]{:S(2)}) async-start(bf16[32,16,1536]{2,1,0:T(8,128)(2,1)} %bitcast.69), calls=%async_computation.1 | async-start | bytes 3145728 | tf_op jit(solution)/shard_map/all_to_all | solution.py:92
  113.7 0.1 convert_element_type.183
  113.8 0.1 copy.17
  113.9 0.0 copy-done.5
  113.9 39.4 %all-to-all-done.1 = bf16[32,16,1536]{2,1,0:T(8,128)(2,1)S(1)} async-done(((bf16[32,16,1536]{2,1,0:T(8,128)(2,1)}), bf16[32,16,1536]{2,1,0:T(8,128)(2,1)S(1)}, u32[]{:S(2)}, u32[]{:S(2)}) %all-to-all-start.1) | async-done | bytes 1572896 | tf_op jit(solution)/shard_map/all_to_all | solution.py:92
  153.3 0.6 fusion.16
  153.9 1.0 fusion.19
  (8 shorter events, 0.1 us)
Async XLA Ops:
  6.5 30.5 %copy-start = (bf16[1,128,1536]{2,1,0:T(8,128)(2,1)S(1)}, bf16[1,128,1536]{2,1,0:T(8,128)(2,1)}, u32[]{:S(2)}) copy-start(bf16[1,128,1536]{2,1,0:T(8,128)(2,1)} %param.10) | copy-start | bytes 1179652
  6.5 31.1 %copy-start.1 = (f32[1536]{0:T(1024)S(1)}, f32[1536]{0:T(1024)}, u32[]{:S(2)}) copy-start(f32[1536]{0:T(1024)} %param.11) | copy-start | bytes 18436
  6.5 31.6 %copy-start.2 = (f32[1536]{0:T(1024)S(1)}, f32[1536]{0:T(1024)}, u32[]{:S(2)}) copy-start(f32[1536]{0:T(1024)} %param.14) | copy-start | bytes 18436
  6.5 31.6 %copy-start.3 = (f32[1536]{0:T(1024)S(1)}, f32[1536]{0:T(1024)}, u32[]{:S(2)}) copy-start(f32[1536]{0:T(1024)} %param.13) | copy-start | bytes 18436
  6.5 89.9 %all-gather.2.cloned.1.call-start = ((), (), s32[]{:S(2)}) async-start(), calls=%async_computation.2 | async-start | bytes 10027008 | tf_op jit(solution)/shard_map/all_gather | solution.py:60
  26.4 10.3 %collective-permute-start = (bf16[15,1536]{1,0:T(8,128)(2,1)S(1)}, bf16[15,1536]{1,0:T(8,128)(2,1)S(1)}, u32[]{:S(2)}, u32[]{:S(2)}) collective-permute-start(bf16[15,1536]{1,0:T(8,128)(2,1)S(1)} %get-tuple-element.38), channel_id=1, source_target_pairs={{0,1},{1,2},{2,3},{3,4},{4,5},{5,6},{6,7},{7,8},{8,9},{9,10},{10,1... | collective-permute-start | bytes 138248 | tf_op jit(solution)/shard_map/ppermute | solution.py:16
  30.7 6.3 %collective-permute-start.1 = (bf16[15,1536]{1,0:T(8,128)(2,1)S(1)}, bf16[15,1536]{1,0:T(8,128)(2,1)S(1)}, u32[]{:S(2)}, u32[]{:S(2)}) collective-permute-start(bf16[15,1536]{1,0:T(8,128)(2,1)S(1)} %get-tuple-element.39), channel_id=1, source_target_pairs={{1,0},{2,1},{3,2},{4,3},{5,4},{6,5},{7,6},{8,7},{9,8},{10,9},{11,1... | collective-permute-start | bytes 138248 | tf_op jit(solution)/shard_map/ppermute | solution.py:19
  38.1 4.0 %copy-start.4 = (f32[1536]{0:T(1024)S(1)}, f32[1536]{0:T(1024)}, u32[]{:S(2)}) copy-start(f32[1536]{0:T(1024)} %param.15) | copy-start | bytes 18436
  106.8 7.1 %copy-start.5 = (f32[1,128,2]{1,2,0:T(2,128)S(1)}, f32[1,128,2]{1,2,0:T(2,128)}, u32[]{:S(2)}) copy-start(f32[1,128,2]{1,2,0:T(2,128)} %param.17) | copy-start | bytes 3076
  106.8 46.5 %all-to-all-start.1 = ((bf16[32,16,1536]{2,1,0:T(8,128)(2,1)}), bf16[32,16,1536]{2,1,0:T(8,128)(2,1)S(1)}, u32[]{:S(2)}, u32[]{:S(2)}) async-start(bf16[32,16,1536]{2,1,0:T(8,128)(2,1)} %bitcast.69), calls=%async_computation.1 | async-start | bytes 3145728 | tf_op jit(solution)/shard_map/all_to_all | solution.py:92
Sparse Core Ops, SparseCore 0:
  25.7 67.2 all-gather.1

commit v5 on v3

--- a/solution.py
+++ b/solution.py
@@ -1,6 +1,8 @@
 import jax
 import jax.numpy as jnp
 from jax import lax
+from jax.experimental import pallas as pl
+from jax.experimental.pallas import tpu as pltpu
 from jax.sharding import PartitionSpec as P
 
 eps_norm = 1e-05
@@ -17,6 +19,46 @@
         high = lax.ppermute(lax.slice_in_dim(block, 0, width, axis=dim), axis, backward)
         block = jnp.concatenate([low, block, high], axis=dim)
     return block
+
+
+def expert_ffn(rows, both, step=256):
+    count, width = rows.shape
+    hidden_units = both.shape[2]
+    steps = hidden_units // step
+
+    def body(x_ref, first_ref, second_ref, out_ref, acc_ref):
+        j = pl.program_id(0)
+
+        @pl.when(j == 0)
+        def _():
+            acc_ref[...] = jnp.zeros_like(acc_ref)
+
+        h = jnp.dot(x_ref[...], first_ref[...], preferred_element_type=jnp.float32)
+        h = (h / (1.0 + jnp.exp(-h))).astype(jnp.bfloat16)
+        acc_ref[...] += jnp.dot(h, second_ref[...], preferred_element_type=jnp.float32)
+
+        @pl.when(j == steps - 1)
+        def _():
+            out_ref[...] = acc_ref[...].astype(out_ref.dtype)
+
+    return pl.pallas_call(
+        body,
+        grid=(steps,),
+        in_specs=[
+            pl.BlockSpec((count, width), lambda j: (0, 0)),
+            pl.BlockSpec((None, width, step), lambda j: (0, 0, j)),
+            pl.BlockSpec((None, step, width), lambda j: (1, j, 0)),
+        ],
+        out_specs=pl.BlockSpec((count, width), lambda j: (0, 0)),
+        out_shape=jax.ShapeDtypeStruct((count, width), jnp.bfloat16),
+        scratch_shapes=[pltpu.VMEM((count, width), jnp.float32)],
+        compiler_params=pltpu.CompilerParams(dimension_semantics=("arbitrary",)),
+        cost_estimate=pl.CostEstimate(
+            flops=4 * count * width * hidden_units,
+            transcendentals=count * hidden_units,
+            bytes_accessed=2 * (2 * count * width + 2 * width * hidden_units),
+        ),
+    )(rows, both, both)
 
 
 def layer_norm(values, gain):
@@ -36,7 +78,6 @@
     capacity = 2 * picks_per * frame_count // experts_all
     slots_all = experts_all * capacity
     both = lax.all_gather(jnp.concatenate([w_in, w_out], axis=0), "fsdp", axis=1, tiled=True)
-    full_in, full_out = both[0:1], both[1:2]
     raw = padded_2(frames[0], (("expert", 0),), reach)
     padded = layer_norm(raw.astype(jnp.float32), ln_gain).astype(jnp.bfloat16)
     stream = frames[0].astype(jnp.float32)
@@ -63,10 +104,7 @@
     outgoing = outgoing.astype(jnp.bfloat16).reshape(experts_all, capacity, width)
     block = lax.all_to_all(outgoing, "expert", split_axis=0, concat_axis=0, tiled=True)
     rows_in = block.reshape(-1, width)
-    hidden = jax.nn.silu(jnp.dot(rows_in, full_in[0], preferred_element_type=jnp.float32)).astype(
-        jnp.bfloat16
-    )
-    result = jnp.dot(hidden, full_out[0], preferred_element_type=jnp.float32).astype(jnp.bfloat16)
+    result = expert_ffn(rows_in, both)
     returned = lax.all_to_all(
         result.reshape(block.shape), "expert", split_axis=0, concat_axis=0, tiled=True
     )

time: 146 us -> 150 us (1.027)
  Pallas kernels: 0 us -> 14.4 us
  matrix products: 11.8 us -> 1.48 us
  local copies, waits for them, and re-layouts: 5.43 us -> 1.22 us
  waiting for transfers between devices: 39.8 us -> 43.6 us
  starting transfers between devices: 13.3 us -> 15.9 us
  blocking collectives: 53.6 us -> 51.3 us
    pallas_call x0 -> x1, Pallas kernels: none -> 14.4 us  [expert_ffn(): pl.pallas_call(body, grid=(steps,), in_specs=[pl.BlockSpec((count, width)...]
    dot_general x1 -> x0, matrix products: 10.3 us -> none  [shards(): jnp.dot(hidden, full_out[0], preferred_element_type=jnp.float32)]
    ppermute x1, waiting for transfers between devices: 0.34 us -> 3.72 us  [padded_2(): lax.ppermute(lax.slice_in_dim(block, 0, width, axis=dim), axis, backward)]
    slice x2, local copies, waits for them, and re-layouts: 3.25 us -> 0.53 us  [shards(): filtered = filtered + kernel[offset] * padded[offset:offset + frame_count]]
    all_to_all x1, starting transfers between devices: 7.68 us -> 10.3 us  [shards(): lax.all_to_all(result.reshape(block.shape), 'expert', split_axis=0, conca...]
    all_to_all x1, blocking collectives: 53.6 us -> 51.3 us  [shards(): lax.all_to_all(outgoing, 'expert', split_axis=0, concat_axis=0, tiled=True)]
  transfers between devices with their start and end apart: 4 -> 4, of which waited for: 2 -> 3; matrix products, arithmetic and copies ran while one was open for 8% -> 5% of each run, Pallas kernels for 0% -> 0%
where the time goes in v5:
time: 150 us
  blocking collectives  51.3 us (34%)
  waiting for transfers between devices  43.6 us (29%)
  starting transfers between devices  15.9 us (11%)
  Pallas kernels  14.4 us (10%)
  between operations  13.6 us (9%)
  other arithmetic  8.02 us (5%)
    all_to_all x1, blocking collectives, shards(): lax.all_to_all(outgoing, 'expert', split_axis=0, concat_axis=0, tiled=True)  51.3 us
    all_to_all x1, waiting for transfers between devices, shards(): lax.all_to_all(result.reshape(block.shape), 'expert', split_axis=0, conca...  39.4 us
    pallas_call x1, Pallas kernels, expert_ffn(): pl.pallas_call(body, grid=(steps,), in_specs=[pl.BlockSpec((count, width)...  14.4 us
    all_to_all x1, starting transfers between devices, shards(): lax.all_to_all(result.reshape(block.shape), 'expert', split_axis=0, conca...  10.3 us
    ppermute x1, starting transfers between devices, padded_2(): lax.ppermute(lax.slice_in_dim(block, block.shape[dim] - width, None, axis...  4.28 us
    reduce_sum x2, other arithmetic, layer_norm(): centre = jnp.mean(values, axis=-1, keepdims=True)  3.96 us
    ppermute x1, waiting for transfers between devices, padded_2(): lax.ppermute(lax.slice_in_dim(block, 0, width, axis=dim), axis, backward)  3.72 us
  transfers between devices with their start and end apart: 4, of which 3 were waited for; matrix products, arithmetic and copies ran while one was open for 5% of the time, Pallas kernels for 0%

profile of v5, /device:TPU:24, one launch (start us, length us, event | category | flops | bytes accessed | tf_op | source)
XLA Modules:
  0.0 149.6 jit_solution(1733634184368878846)
XLA Ops:
  6.5 0.0 copy-start
  6.5 0.0 copy-start.6
  6.5 0.0 copy-start.1
  6.5 0.0 all-gather.2.cloned.1.call-start
  6.5 2.0 %pad_maximum_fusion = bf16[2,96,1536]{2,1,0:T(8,128)(2,1)} fusion(bf16[1,96,1536]{2,1,0:T(8,128)(2,1)} %param.19, bf16[1,96,1536]{2,1,0:T(8,128)(2,1)} %param.18), kind=kLoop, calls=%fused_computation.21 | loop fusion | flops 294912 | bytes 1179648 | tf_op jit(solution)/shard_map/concatenate | solution.py:80
  8.5 0.0 copy-start.2
  8.5 0.0 all-gather.2.cloned.1.call-update
  8.6 0.0 copy-done
  8.6 0.0 copy-start.3
  8.6 0.0 copy-start.4
  8.6 4.3 %collective-permute-start = (bf16[15,1536]{1,0:T(8,128)(2,1)S(1)}, bf16[15,1536]{1,0:T(8,128)(2,1)S(1)}, u32[]{:S(2)}, u32[]{:S(2)}) collective-permute-start(bf16[15,1536]{1,0:T(8,128)(2,1)S(1)} %get-tuple-element.38), channel_id=1, source_target_pairs={{0,1},{1,2},{2,3},{3,4},{4,5},{5,6},{6,7},{7,8},{8,9},{9,10},{10,1... | collective-permute-start | bytes 138248 | tf_op jit(solution)/shard_map/ppermute | solution.py:16
  12.9 1.3 collective-permute-start.1
  14.2 0.0 copy-done.6
  14.2 0.1 copy.15
  14.3 0.1 eq.59
  14.5 0.2 fusion.2
  14.7 0.1 convert_element_type.178
  14.9 0.1 copy.18
  14.9 0.0 copy-done.1
  14.9 0.2 slice_reduce_fusion.29
  15.1 0.3 slice_reduce_fusion.30
  15.5 0.1 fusion.15
  15.5 0.0 collective-permute-done
  15.5 3.7 %collective-permute-done.1 = bf16[15,1536]{1,0:T(8,128)(2,1)S(1)} collective-permute-done((bf16[15,1536]{1,0:T(8,128)(2,1)S(1)}, bf16[15,1536]{1,0:T(8,128)(2,1)S(1)}, u32[]{:S(2)}, u32[]{:S(2)}) %collective-permute-start.1) | collective-permute-done | bytes 46112 | tf_op jit(solution)/shard_map/ppermute | solution.py:19
  19.2 0.2 convert_reduce_fusion
  19.5 0.3 fusion.3
  19.8 0.0 copy-done.2
  19.8 0.4 fusion.5
  20.3 0.0 copy-done.3
  20.3 0.0 copy-done.4
  20.3 0.0 copy-start.5
  20.3 3.7 %fusion.23 = (f32[128]{0:T(128)S(1)}, f32[128,1536]{1,0:T(8,128)S(1)}) fusion(f32[1536]{0:T(1024)S(1)} %copy-done.3, bf16[158,1536]{1,0:T(8,128)(2,1)S(1)} %fusion.5, f32[1536]{0:T(1024)S(1)} %get-tuple-element.34, f32[1536]{0:T(1024)S(1)} %get-tuple-element.35, f32[1536]{0:T(1024)S(1)} %get-tuple-element.6, f32[1536]{0:T(1024)S(1)} %get-tuple-element.7, ...), kind=kLoop, calls=%fused_computation.78 | loop fusion | flops 19857280 | bytes 13572608 | tf_op jit(solution)/shard_map/reduce_sum | solution.py:65
  24.1 0.2 multiply_reduce_fusion
  24.3 0.0 copy-done.5
  24.3 0.7 convolution_convert_fusion
  25.0 51.3 %all_to_all.10 = bf16[32,16,1536]{2,1,0:T(8,128)(2,1)} all-to-all(bf16[32,16,1536]{2,1,0:T(8,128)(2,1)S(1)} %bitcast.55), channel_id=1, replica_groups=mesh['fsdp'=16,'expert'=32] {'expert'}, dimensions={0} | all-to-all | bytes 3145728 | tf_op jit(solution)/shard_map/all_to_all | solution.py:105
  76.3 0.5 all-gather.2.cloned.1.call-done.first_ref.second_ref
  76.8 14.4 %shard_map.100 = bf16[512,1536]{1,0:T(8,128)(2,1)} custom-call(bf16[512,1536]{1,0:T(8,128)(2,1)} %bitcast.57, bf16[2,1536,1536]{2,1,0:T(8,128)(2,1)} %all-gather.2.cloned.1.call-done.first_ref.second_ref, bf16[2,1536,1536]{2,1,0:T(8,128)(2,1)} %all-gather.2.cloned.1.call-done.first_ref.second_ref), custom_call_target="tpu_custom_call" | custom-call | flops 4831838208 | bytes 12582912 | tf_op jit(solution)/shard_map/pallas_call | solution.py:44
  91.2 0.0 copy-start.7
  91.2 10.3 %all-to-all-start.1 = ((bf16[32,16,1536]{2,1,0:T(8,128)(2,1)}), bf16[32,16,1536]{2,1,0:T(8,128)(2,1)S(1)}, u32[]{:S(2)}, u32[]{:S(2)}) async-start(bf16[32,16,1536]{2,1,0:T(8,128)(2,1)} %bitcast.56), calls=%async_computation.1 | async-start | bytes 3145728 | tf_op jit(solution)/shard_map/all_to_all | solution.py:108
  101.5 0.1 convert_element_type.177
  101.7 0.1 copy.17
  101.7 0.0 copy-done.7
  101.8 39.4 %all-to-all-done.1 = bf16[32,16,1536]{2,1,0:T(8,128)(2,1)S(1)} async-done(((bf16[32,16,1536]{2,1,0:T(8,128)(2,1)}), bf16[32,16,1536]{2,1,0:T(8,128)(2,1)S(1)}, u32[]{:S(2)}, u32[]{:S(2)}) %all-to-all-start.1) | async-done | bytes 1572896 | tf_op jit(solution)/shard_map/all_to_all | solution.py:108
  141.2 0.6 fusion.13
  141.8 1.0 fusion.16
  (9 shorter events, 0.1 us)
Async XLA Ops:
  6.5 2.0 %copy-start = (bf16[1,128,1536]{2,1,0:T(8,128)(2,1)S(1)}, bf16[1,128,1536]{2,1,0:T(8,128)(2,1)}, u32[]{:S(2)}) copy-start(bf16[1,128,1536]{2,1,0:T(8,128)(2,1)} %param.10) | copy-start | bytes 1179652
  6.5 7.7 %copy-start.6 = (s32[1,128,2]{1,2,0:T(2,128)S(1)}, s32[1,128,2]{1,2,0:T(2,128)}, u32[]{:S(2)}) copy-start(s32[1,128,2]{1,2,0:T(2,128)} %param.16) | copy-start | bytes 3076
  6.5 8.4 %copy-start.1 = (f32[31,1536]{1,0:T(8,128)S(1)}, f32[31,1536]{1,0:T(8,128)}, u32[]{:S(2)}) copy-start(f32[31,1536]{1,0:T(8,128)} %param.12) | copy-start | bytes 571396
  6.5 70.2 %all-gather.2.cloned.1.call-start = ((), (), s32[]{:S(2)}) async-start(), calls=%async_computation.2 | async-start | bytes 10027008 | tf_op jit(solution)/shard_map/all_gather | solution.py:80
  8.5 11.3 %copy-start.2 = (f32[1536]{0:T(1024)S(1)}, f32[1536]{0:T(1024)}, u32[]{:S(2)}) copy-start(f32[1536]{0:T(1024)} %param.11) | copy-start | bytes 18436
  8.6 11.7 %copy-start.3 = (f32[1536]{0:T(1024)S(1)}, f32[1536]{0:T(1024)}, u32[]{:S(2)}) copy-start(f32[1536]{0:T(1024)} %param.14) | copy-start | bytes 18436
  8.6 11.7 %copy-start.4 = (f32[1536]{0:T(1024)S(1)}, f32[1536]{0:T(1024)}, u32[]{:S(2)}) copy-start(f32[1536]{0:T(1024)} %param.13) | copy-start | bytes 18436
  8.6 6.9 %collective-permute-start = (bf16[15,1536]{1,0:T(8,128)(2,1)S(1)}, bf16[15,1536]{1,0:T(8,128)(2,1)S(1)}, u32[]{:S(2)}, u32[]{:S(2)}) collective-permute-start(bf16[15,1536]{1,0:T(8,128)(2,1)S(1)} %get-tuple-element.38), channel_id=1, source_target_pairs={{0,1},{1,2},{2,3},{3,4},{4,5},{5,6},{6,7},{7,8},{8,9},{9,10},{10,1... | collective-permute-start | bytes 138248 | tf_op jit(solution)/shard_map/ppermute | solution.py:16
  12.9 6.3 %collective-permute-start.1 = (bf16[15,1536]{1,0:T(8,128)(2,1)S(1)}, bf16[15,1536]{1,0:T(8,128)(2,1)S(1)}, u32[]{:S(2)}, u32[]{:S(2)}) collective-permute-start(bf16[15,1536]{1,0:T(8,128)(2,1)S(1)} %get-tuple-element.39), channel_id=1, source_target_pairs={{1,0},{2,1},{3,2},{4,3},{5,4},{6,5},{7,6},{8,7},{9,8},{10,9},{11,1... | collective-permute-start | bytes 138248 | tf_op jit(solution)/shard_map/ppermute | solution.py:19
  20.3 4.0 %copy-start.5 = (f32[1536]{0:T(1024)S(1)}, f32[1536]{0:T(1024)}, u32[]{:S(2)}) copy-start(f32[1536]{0:T(1024)} %param.15) | copy-start | bytes 18436
  91.2 10.5 %copy-start.7 = (f32[1,128,2]{1,2,0:T(2,128)S(1)}, f32[1,128,2]{1,2,0:T(2,128)}, u32[]{:S(2)}) copy-start(f32[1,128,2]{1,2,0:T(2,128)} %param.17) | copy-start | bytes 3076
  91.2 50.0 %all-to-all-start.1 = ((bf16[32,16,1536]{2,1,0:T(8,128)(2,1)}), bf16[32,16,1536]{2,1,0:T(8,128)(2,1)S(1)}, u32[]{:S(2)}, u32[]{:S(2)}) async-start(bf16[32,16,1536]{2,1,0:T(8,128)(2,1)} %bitcast.56), calls=%async_computation.1 | async-start | bytes 3145728 | tf_op jit(solution)/shard_map/all_to_all | solution.py:108
Sparse Core Ops, SparseCore 0:
  9.5 67.2 all-gather.1

commit v6 on v5

--- a/solution.py
+++ b/solution.py
@@ -21,7 +21,7 @@
     return block
 
 
-def expert_ffn(rows, both, step=256):
+def expert_ffn(rows, both, step=512):
     count, width = rows.shape
     hidden_units = both.shape[2]
     steps = hidden_units // step

time: 150 us -> 146 us (0.973)
  Pallas kernels: 14.4 us -> 10.2 us
    pallas_call x1, Pallas kernels: 14.4 us -> 10.2 us  [expert_ffn(): pl.pallas_call(body, grid=(steps,), in_specs=[pl.BlockSpec((count, width)...]
where the time goes in v6:
time: 146 us; the launch traced here: 145 us
  blocking collectives  51.3 us (35%)
  waiting for transfers between devices  43.6 us (30%)
  starting transfers between devices  15.9 us (11%)
  between operations  13.6 us (9%)
  Pallas kernels  10.2 us (7%)
  other arithmetic  8.02 us (5%)
  matrix products  1.48 us (1%)
    all_to_all x1, blocking collectives, shards(): lax.all_to_all(outgoing, 'expert', split_axis=0, concat_axis=0, tiled=True)  51.3 us
    all_to_all x1, waiting for transfers between devices, shards(): lax.all_to_all(result.reshape(block.shape), 'expert', split_axis=0, conca...  39.4 us
    all_to_all x1, starting transfers between devices, shards(): lax.all_to_all(result.reshape(block.shape), 'expert', split_axis=0, conca...  10.3 us
    pallas_call x1, Pallas kernels, expert_ffn(): pl.pallas_call(body, grid=(steps,), in_specs=[pl.BlockSpec((count, width)...  10.2 us
    ppermute x1, starting transfers between devices, padded_2(): lax.ppermute(lax.slice_in_dim(block, block.shape[dim] - width, None, axis...  4.28 us
    reduce_sum x2, other arithmetic, layer_norm(): centre = jnp.mean(values, axis=-1, keepdims=True)  3.96 us
    ppermute x1, waiting for transfers between devices, padded_2(): lax.ppermute(lax.slice_in_dim(block, 0, width, axis=dim), axis, backward)  3.72 us
  transfers between devices with their start and end apart: 4, of which 3 were waited for; matrix products, arithmetic and copies ran while one was open for 5% of the time, Pallas kernels for 0%

profile of v6, /device:TPU:24, one launch (start us, length us, event | category | flops | bytes accessed | tf_op | source)
XLA Modules:
  0.0 145.4 jit_solution(7442531082342959773)
XLA Ops:
  6.5 0.0 copy-start
  6.5 0.0 copy-start.6
  6.5 0.0 copy-start.1
  6.5 0.0 all-gather.2.cloned.1.call-start
  6.5 2.0 %pad_maximum_fusion = bf16[2,96,1536]{2,1,0:T(8,128)(2,1)} fusion(bf16[1,96,1536]{2,1,0:T(8,128)(2,1)} %param.19, bf16[1,96,1536]{2,1,0:T(8,128)(2,1)} %param.18), kind=kLoop, calls=%fused_computation.21 | loop fusion | flops 294912 | bytes 1179648 | tf_op jit(solution)/shard_map/concatenate | solution.py:80
  8.5 0.0 copy-start.2
  8.5 0.0 all-gather.2.cloned.1.call-update
  8.6 0.0 copy-done
  8.6 0.0 copy-start.3
  8.6 0.0 copy-start.4
  8.6 4.3 %collective-permute-start = (bf16[15,1536]{1,0:T(8,128)(2,1)S(1)}, bf16[15,1536]{1,0:T(8,128)(2,1)S(1)}, u32[]{:S(2)}, u32[]{:S(2)}) collective-permute-start(bf16[15,1536]{1,0:T(8,128)(2,1)S(1)} %get-tuple-element.38), channel_id=1, source_target_pairs={{0,1},{1,2},{2,3},{3,4},{4,5},{5,6},{6,7},{7,8},{8,9},{9,10},{10,1... | collective-permute-start | bytes 138248 | tf_op jit(solution)/shard_map/ppermute | solution.py:16
  12.9 1.3 collective-permute-start.1
  14.2 0.0 copy-done.6
  14.2 0.1 copy.15
  14.3 0.1 eq.59
  14.5 0.2 fusion.2
  14.7 0.1 convert_element_type.178
  14.9 0.1 copy.18
  14.9 0.0 copy-done.1
  14.9 0.2 slice_reduce_fusion.29
  15.1 0.3 slice_reduce_fusion.30
  15.5 0.1 fusion.15
  15.5 0.0 collective-permute-done
  15.5 3.7 %collective-permute-done.1 = bf16[15,1536]{1,0:T(8,128)(2,1)S(1)} collective-permute-done((bf16[15,1536]{1,0:T(8,128)(2,1)S(1)}, bf16[15,1536]{1,0:T(8,128)(2,1)S(1)}, u32[]{:S(2)}, u32[]{:S(2)}) %collective-permute-start.1) | collective-permute-done | bytes 46112 | tf_op jit(solution)/shard_map/ppermute | solution.py:19
  19.2 0.2 convert_reduce_fusion
  19.5 0.3 fusion.3
  19.8 0.0 copy-done.2
  19.8 0.4 fusion.5
  20.3 0.0 copy-done.3
  20.3 0.0 copy-done.4
  20.3 0.0 copy-start.5
  20.3 3.7 %fusion.23 = (f32[128]{0:T(128)S(1)}, f32[128,1536]{1,0:T(8,128)S(1)}) fusion(f32[1536]{0:T(1024)S(1)} %copy-done.3, bf16[158,1536]{1,0:T(8,128)(2,1)S(1)} %fusion.5, f32[1536]{0:T(1024)S(1)} %get-tuple-element.34, f32[1536]{0:T(1024)S(1)} %get-tuple-element.35, f32[1536]{0:T(1024)S(1)} %get-tuple-element.6, f32[1536]{0:T(1024)S(1)} %get-tuple-element.7, ...), kind=kLoop, calls=%fused_computation.78 | loop fusion | flops 19857280 | bytes 13572608 | tf_op jit(solution)/shard_map/reduce_sum | solution.py:65
  24.1 0.2 multiply_reduce_fusion
  24.3 0.0 copy-done.5
  24.3 0.7 convolution_convert_fusion
  25.0 51.3 %all_to_all.10 = bf16[32,16,1536]{2,1,0:T(8,128)(2,1)} all-to-all(bf16[32,16,1536]{2,1,0:T(8,128)(2,1)S(1)} %bitcast.55), channel_id=1, replica_groups=mesh['fsdp'=16,'expert'=32] {'expert'}, dimensions={0} | all-to-all | bytes 3145728 | tf_op jit(solution)/shard_map/all_to_all | solution.py:105
  76.3 0.5 all-gather.2.cloned.1.call-done.first_ref.second_ref
  76.8 10.2 %shard_map.100 = bf16[512,1536]{1,0:T(8,128)(2,1)} custom-call(bf16[512,1536]{1,0:T(8,128)(2,1)} %bitcast.57, bf16[2,1536,1536]{2,1,0:T(8,128)(2,1)} %all-gather.2.cloned.1.call-done.first_ref.second_ref, bf16[2,1536,1536]{2,1,0:T(8,128)(2,1)} %all-gather.2.cloned.1.call-done.first_ref.second_ref), custom_call_target="tpu_custom_call" | custom-call | flops 4831838208 | bytes 12582912 | tf_op jit(solution)/shard_map/pallas_call | solution.py:44
  87.0 0.0 copy-start.7
  87.0 10.3 %all-to-all-start.1 = ((bf16[32,16,1536]{2,1,0:T(8,128)(2,1)}), bf16[32,16,1536]{2,1,0:T(8,128)(2,1)S(1)}, u32[]{:S(2)}, u32[]{:S(2)}) async-start(bf16[32,16,1536]{2,1,0:T(8,128)(2,1)} %bitcast.56), calls=%async_computation.1 | async-start | bytes 3145728 | tf_op jit(solution)/shard_map/all_to_all | solution.py:108
  97.3 0.1 convert_element_type.177
  97.5 0.1 copy.17
  97.5 0.0 copy-done.7
  97.5 39.4 %all-to-all-done.1 = bf16[32,16,1536]{2,1,0:T(8,128)(2,1)S(1)} async-done(((bf16[32,16,1536]{2,1,0:T(8,128)(2,1)}), bf16[32,16,1536]{2,1,0:T(8,128)(2,1)S(1)}, u32[]{:S(2)}, u32[]{:S(2)}) %all-to-all-start.1) | async-done | bytes 1572896 | tf_op jit(solution)/shard_map/all_to_all | solution.py:108
  137.0 0.6 fusion.13
  137.6 1.0 fusion.16
  (9 shorter events, 0.1 us)
Async XLA Ops:
  6.5 2.0 %copy-start = (bf16[1,128,1536]{2,1,0:T(8,128)(2,1)S(1)}, bf16[1,128,1536]{2,1,0:T(8,128)(2,1)}, u32[]{:S(2)}) copy-start(bf16[1,128,1536]{2,1,0:T(8,128)(2,1)} %param.10) | copy-start | bytes 1179652
  6.5 7.7 %copy-start.6 = (s32[1,128,2]{1,2,0:T(2,128)S(1)}, s32[1,128,2]{1,2,0:T(2,128)}, u32[]{:S(2)}) copy-start(s32[1,128,2]{1,2,0:T(2,128)} %param.16) | copy-start | bytes 3076
  6.5 8.4 %copy-start.1 = (f32[31,1536]{1,0:T(8,128)S(1)}, f32[31,1536]{1,0:T(8,128)}, u32[]{:S(2)}) copy-start(f32[31,1536]{1,0:T(8,128)} %param.12) | copy-start | bytes 571396
  6.5 70.2 %all-gather.2.cloned.1.call-start = ((), (), s32[]{:S(2)}) async-start(), calls=%async_computation.2 | async-start | bytes 10027008 | tf_op jit(solution)/shard_map/all_gather | solution.py:80
  8.5 11.3 %copy-start.2 = (f32[1536]{0:T(1024)S(1)}, f32[1536]{0:T(1024)}, u32[]{:S(2)}) copy-start(f32[1536]{0:T(1024)} %param.11) | copy-start | bytes 18436
  8.6 11.7 %copy-start.3 = (f32[1536]{0:T(1024)S(1)}, f32[1536]{0:T(1024)}, u32[]{:S(2)}) copy-start(f32[1536]{0:T(1024)} %param.14) | copy-start | bytes 18436
  8.6 11.7 %copy-start.4 = (f32[1536]{0:T(1024)S(1)}, f32[1536]{0:T(1024)}, u32[]{:S(2)}) copy-start(f32[1536]{0:T(1024)} %param.13) | copy-start | bytes 18436
  8.6 6.9 %collective-permute-start = (bf16[15,1536]{1,0:T(8,128)(2,1)S(1)}, bf16[15,1536]{1,0:T(8,128)(2,1)S(1)}, u32[]{:S(2)}, u32[]{:S(2)}) collective-permute-start(bf16[15,1536]{1,0:T(8,128)(2,1)S(1)} %get-tuple-element.38), channel_id=1, source_target_pairs={{0,1},{1,2},{2,3},{3,4},{4,5},{5,6},{6,7},{7,8},{8,9},{9,10},{10,1... | collective-permute-start | bytes 138248 | tf_op jit(solution)/shard_map/ppermute | solution.py:16
  12.9 6.3 %collective-permute-start.1 = (bf16[15,1536]{1,0:T(8,128)(2,1)S(1)}, bf16[15,1536]{1,0:T(8,128)(2,1)S(1)}, u32[]{:S(2)}, u32[]{:S(2)}) collective-permute-start(bf16[15,1536]{1,0:T(8,128)(2,1)S(1)} %get-tuple-element.39), channel_id=1, source_target_pairs={{1,0},{2,1},{3,2},{4,3},{5,4},{6,5},{7,6},{8,7},{9,8},{10,9},{11,1... | collective-permute-start | bytes 138248 | tf_op jit(solution)/shard_map/ppermute | solution.py:19
  20.3 4.0 %copy-start.5 = (f32[1536]{0:T(1024)S(1)}, f32[1536]{0:T(1024)}, u32[]{:S(2)}) copy-start(f32[1536]{0:T(1024)} %param.15) | copy-start | bytes 18436
  87.0 10.5 %copy-start.7 = (f32[1,128,2]{1,2,0:T(2,128)S(1)}, f32[1,128,2]{1,2,0:T(2,128)}, u32[]{:S(2)}) copy-start(f32[1,128,2]{1,2,0:T(2,128)} %param.17) | copy-start | bytes 3076
  87.0 50.0 %all-to-all-start.1 = ((bf16[32,16,1536]{2,1,0:T(8,128)(2,1)}), bf16[32,16,1536]{2,1,0:T(8,128)(2,1)S(1)}, u32[]{:S(2)}, u32[]{:S(2)}) async-start(bf16[32,16,1536]{2,1,0:T(8,128)(2,1)} %bitcast.56), calls=%async_computation.1 | async-start | bytes 3145728 | tf_op jit(solution)/shard_map/all_to_all | solution.py:108
Sparse Core Ops, SparseCore 0:
  9.5 67.2 all-gather.1

commit v7 on v6

--- a/solution.py
+++ b/solution.py
@@ -21,7 +21,7 @@
     return block
 
 
-def expert_ffn(rows, both, step=512):
+def expert_ffn(rows, both, step=768):
     count, width = rows.shape
     hidden_units = both.shape[2]
     steps = hidden_units // step

time: 146 us -> 147 us (level)
  no operation moved by 1% of the time
where the time goes in v7:
time: 147 us
  blocking collectives  51.3 us (35%)
  waiting for transfers between devices  43.6 us (30%)
  starting transfers between devices  15.9 us (11%)
  between operations  13.6 us (9%)
  Pallas kernels  11.5 us (8%)
  other arithmetic  8.02 us (5%)
  matrix products  1.48 us (1%)
    all_to_all x1, blocking collectives, shards(): lax.all_to_all(outgoing, 'expert', split_axis=0, concat_axis=0, tiled=True)  51.3 us
    all_to_all x1, waiting for transfers between devices, shards(): lax.all_to_all(result.reshape(block.shape), 'expert', split_axis=0, conca...  39.4 us
    pallas_call x1, Pallas kernels, expert_ffn(): pl.pallas_call(body, grid=(steps,), in_specs=[pl.BlockSpec((count, width)...  11.5 us
    all_to_all x1, starting transfers between devices, shards(): lax.all_to_all(result.reshape(block.shape), 'expert', split_axis=0, conca...  10.3 us
    ppermute x1, starting transfers between devices, padded_2(): lax.ppermute(lax.slice_in_dim(block, block.shape[dim] - width, None, axis...  4.28 us
    reduce_sum x2, other arithmetic, layer_norm(): centre = jnp.mean(values, axis=-1, keepdims=True)  3.96 us
    ppermute x1, waiting for transfers between devices, padded_2(): lax.ppermute(lax.slice_in_dim(block, 0, width, axis=dim), axis, backward)  3.72 us
  transfers between devices with their start and end apart: 4, of which 3 were waited for; matrix products, arithmetic and copies ran while one was open for 5% of the time, Pallas kernels for 0%

profile of v7, /device:TPU:24, one launch (start us, length us, event | category | flops | bytes accessed | tf_op | source)
XLA Modules:
  0.0 146.6 jit_solution(8382031112419639931)
XLA Ops:
  6.5 0.0 copy-start
  6.5 0.0 copy-start.6
  6.5 0.0 copy-start.1
  6.5 0.0 all-gather.2.cloned.1.call-start
  6.5 2.0 %pad_maximum_fusion = bf16[2,96,1536]{2,1,0:T(8,128)(2,1)} fusion(bf16[1,96,1536]{2,1,0:T(8,128)(2,1)} %param.19, bf16[1,96,1536]{2,1,0:T(8,128)(2,1)} %param.18), kind=kLoop, calls=%fused_computation.21 | loop fusion | flops 294912 | bytes 1179648 | tf_op jit(solution)/shard_map/concatenate | solution.py:80
  8.5 0.0 copy-start.2
  8.5 0.0 all-gather.2.cloned.1.call-update
  8.6 0.0 copy-done
  8.6 0.0 copy-start.3
  8.6 0.0 copy-start.4
  8.6 4.3 %collective-permute-start = (bf16[15,1536]{1,0:T(8,128)(2,1)S(1)}, bf16[15,1536]{1,0:T(8,128)(2,1)S(1)}, u32[]{:S(2)}, u32[]{:S(2)}) collective-permute-start(bf16[15,1536]{1,0:T(8,128)(2,1)S(1)} %get-tuple-element.38), channel_id=1, source_target_pairs={{0,1},{1,2},{2,3},{3,4},{4,5},{5,6},{6,7},{7,8},{8,9},{9,10},{10,1... | collective-permute-start | bytes 138248 | tf_op jit(solution)/shard_map/ppermute | solution.py:16
  12.9 1.3 collective-permute-start.1
  14.2 0.0 copy-done.6
  14.2 0.1 copy.15
  14.3 0.1 eq.59
  14.5 0.2 fusion.2
  14.7 0.1 convert_element_type.178
  14.9 0.1 copy.18
  14.9 0.0 copy-done.1
  14.9 0.2 slice_reduce_fusion.29
  15.1 0.3 slice_reduce_fusion.30
  15.5 0.1 fusion.15
  15.5 0.0 collective-permute-done
  15.5 3.7 %collective-permute-done.1 = bf16[15,1536]{1,0:T(8,128)(2,1)S(1)} collective-permute-done((bf16[15,1536]{1,0:T(8,128)(2,1)S(1)}, bf16[15,1536]{1,0:T(8,128)(2,1)S(1)}, u32[]{:S(2)}, u32[]{:S(2)}) %collective-permute-start.1) | collective-permute-done | bytes 46112 | tf_op jit(solution)/shard_map/ppermute | solution.py:19
  19.2 0.2 convert_reduce_fusion
  19.5 0.3 fusion.3
  19.8 0.0 copy-done.2
  19.8 0.4 fusion.5
  20.3 0.0 copy-done.3
  20.3 0.0 copy-done.4
  20.3 0.0 copy-start.5
  20.3 3.7 %fusion.23 = (f32[128]{0:T(128)S(1)}, f32[128,1536]{1,0:T(8,128)S(1)}) fusion(f32[1536]{0:T(1024)S(1)} %copy-done.3, bf16[158,1536]{1,0:T(8,128)(2,1)S(1)} %fusion.5, f32[1536]{0:T(1024)S(1)} %get-tuple-element.34, f32[1536]{0:T(1024)S(1)} %get-tuple-element.35, f32[1536]{0:T(1024)S(1)} %get-tuple-element.6, f32[1536]{0:T(1024)S(1)} %get-tuple-element.7, ...), kind=kLoop, calls=%fused_computation.78 | loop fusion | flops 19857280 | bytes 13572608 | tf_op jit(solution)/shard_map/reduce_sum | solution.py:65
  24.1 0.2 multiply_reduce_fusion
  24.3 0.0 copy-done.5
  24.3 0.7 convolution_convert_fusion
  25.0 51.3 %all_to_all.10 = bf16[32,16,1536]{2,1,0:T(8,128)(2,1)} all-to-all(bf16[32,16,1536]{2,1,0:T(8,128)(2,1)S(1)} %bitcast.55), channel_id=1, replica_groups=mesh['fsdp'=16,'expert'=32] {'expert'}, dimensions={0} | all-to-all | bytes 3145728 | tf_op jit(solution)/shard_map/all_to_all | solution.py:105
  76.3 0.5 all-gather.2.cloned.1.call-done.first_ref.second_ref
  76.8 11.5 %shard_map.100 = bf16[512,1536]{1,0:T(8,128)(2,1)} custom-call(bf16[512,1536]{1,0:T(8,128)(2,1)} %bitcast.57, bf16[2,1536,1536]{2,1,0:T(8,128)(2,1)} %all-gather.2.cloned.1.call-done.first_ref.second_ref, bf16[2,1536,1536]{2,1,0:T(8,128)(2,1)} %all-gather.2.cloned.1.call-done.first_ref.second_ref), custom_call_target="tpu_custom_call" | custom-call | flops 4831838208 | bytes 12582912 | tf_op jit(solution)/shard_map/pallas_call | solution.py:44
  88.2 0.0 copy-start.7
  88.2 10.3 %all-to-all-start.1 = ((bf16[32,16,1536]{2,1,0:T(8,128)(2,1)}), bf16[32,16,1536]{2,1,0:T(8,128)(2,1)S(1)}, u32[]{:S(2)}, u32[]{:S(2)}) async-start(bf16[32,16,1536]{2,1,0:T(8,128)(2,1)} %bitcast.56), calls=%async_computation.1 | async-start | bytes 3145728 | tf_op jit(solution)/shard_map/all_to_all | solution.py:108
  98.5 0.1 convert_element_type.177
  98.7 0.1 copy.17
  98.8 0.0 copy-done.7
  98.8 39.4 %all-to-all-done.1 = bf16[32,16,1536]{2,1,0:T(8,128)(2,1)S(1)} async-done(((bf16[32,16,1536]{2,1,0:T(8,128)(2,1)}), bf16[32,16,1536]{2,1,0:T(8,128)(2,1)S(1)}, u32[]{:S(2)}, u32[]{:S(2)}) %all-to-all-start.1) | async-done | bytes 1572896 | tf_op jit(solution)/shard_map/all_to_all | solution.py:108
  138.2 0.6 fusion.13
  138.8 1.0 fusion.16
  (9 shorter events, 0.1 us)
Async XLA Ops:
  6.5 2.0 %copy-start = (bf16[1,128,1536]{2,1,0:T(8,128)(2,1)S(1)}, bf16[1,128,1536]{2,1,0:T(8,128)(2,1)}, u32[]{:S(2)}) copy-start(bf16[1,128,1536]{2,1,0:T(8,128)(2,1)} %param.10) | copy-start | bytes 1179652
  6.5 7.7 %copy-start.6 = (s32[1,128,2]{1,2,0:T(2,128)S(1)}, s32[1,128,2]{1,2,0:T(2,128)}, u32[]{:S(2)}) copy-start(s32[1,128,2]{1,2,0:T(2,128)} %param.16) | copy-start | bytes 3076
  6.5 8.4 %copy-start.1 = (f32[31,1536]{1,0:T(8,128)S(1)}, f32[31,1536]{1,0:T(8,128)}, u32[]{:S(2)}) copy-start(f32[31,1536]{1,0:T(8,128)} %param.12) | copy-start | bytes 571396
  6.5 70.2 %all-gather.2.cloned.1.call-start = ((), (), s32[]{:S(2)}) async-start(), calls=%async_computation.2 | async-start | bytes 10027008 | tf_op jit(solution)/shard_map/all_gather | solution.py:80
  8.5 11.3 %copy-start.2 = (f32[1536]{0:T(1024)S(1)}, f32[1536]{0:T(1024)}, u32[]{:S(2)}) copy-start(f32[1536]{0:T(1024)} %param.11) | copy-start | bytes 18436
  8.6 11.7 %copy-start.3 = (f32[1536]{0:T(1024)S(1)}, f32[1536]{0:T(1024)}, u32[]{:S(2)}) copy-start(f32[1536]{0:T(1024)} %param.14) | copy-start | bytes 18436
  8.6 11.7 %copy-start.4 = (f32[1536]{0:T(1024)S(1)}, f32[1536]{0:T(1024)}, u32[]{:S(2)}) copy-start(f32[1536]{0:T(1024)} %param.13) | copy-start | bytes 18436
  8.6 6.9 %collective-permute-start = (bf16[15,1536]{1,0:T(8,128)(2,1)S(1)}, bf16[15,1536]{1,0:T(8,128)(2,1)S(1)}, u32[]{:S(2)}, u32[]{:S(2)}) collective-permute-start(bf16[15,1536]{1,0:T(8,128)(2,1)S(1)} %get-tuple-element.38), channel_id=1, source_target_pairs={{0,1},{1,2},{2,3},{3,4},{4,5},{5,6},{6,7},{7,8},{8,9},{9,10},{10,1... | collective-permute-start | bytes 138248 | tf_op jit(solution)/shard_map/ppermute | solution.py:16
  12.9 6.3 %collective-permute-start.1 = (bf16[15,1536]{1,0:T(8,128)(2,1)S(1)}, bf16[15,1536]{1,0:T(8,128)(2,1)S(1)}, u32[]{:S(2)}, u32[]{:S(2)}) collective-permute-start(bf16[15,1536]{1,0:T(8,128)(2,1)S(1)} %get-tuple-element.39), channel_id=1, source_target_pairs={{1,0},{2,1},{3,2},{4,3},{5,4},{6,5},{7,6},{8,7},{9,8},{10,9},{11,1... | collective-permute-start | bytes 138248 | tf_op jit(solution)/shard_map/ppermute | solution.py:19
  20.3 4.0 %copy-start.5 = (f32[1536]{0:T(1024)S(1)}, f32[1536]{0:T(1024)}, u32[]{:S(2)}) copy-start(f32[1536]{0:T(1024)} %param.15) | copy-start | bytes 18436
  88.2 10.5 %copy-start.7 = (f32[1,128,2]{1,2,0:T(2,128)S(1)}, f32[1,128,2]{1,2,0:T(2,128)}, u32[]{:S(2)}) copy-start(f32[1,128,2]{1,2,0:T(2,128)} %param.17) | copy-start | bytes 3076
  88.2 50.0 %all-to-all-start.1 = ((bf16[32,16,1536]{2,1,0:T(8,128)(2,1)}), bf16[32,16,1536]{2,1,0:T(8,128)(2,1)S(1)}, u32[]{:S(2)}, u32[]{:S(2)}) async-start(bf16[32,16,1536]{2,1,0:T(8,128)(2,1)} %bitcast.56), calls=%async_computation.1 | async-start | bytes 3145728 | tf_op jit(solution)/shard_map/all_to_all | solution.py:108
Sparse Core Ops, SparseCore 0:
  9.5 67.2 all-gather.1

commit v8 on v6

--- a/solution.py
+++ b/solution.py
@@ -61,6 +61,16 @@
     )(rows, both, both)
 
 
+def stack_pair(first, second):
+    def body(first_ref, second_ref, out_ref):
+        out_ref[0] = first_ref[0]
+        out_ref[1] = second_ref[0]
+
+    return pl.pallas_call(
+        body, out_shape=jax.ShapeDtypeStruct((2,) + first.shape[1:], first.dtype)
+    )(first, second)
+
+
 def layer_norm(values, gain):
     centre = jnp.mean(values, axis=-1, keepdims=True)
     centred = values - centre
@@ -77,10 +87,14 @@
     experts_all = lax.axis_size("expert") * w_in.shape[0]
     capacity = 2 * picks_per * frame_count // experts_all
     slots_all = experts_all * capacity
-    both = lax.all_gather(jnp.concatenate([w_in, w_out], axis=0), "fsdp", axis=1, tiled=True)
+    both = lax.all_gather(stack_pair(w_in, w_out), "fsdp", axis=1, tiled=True)
     raw = padded_2(frames[0], (("expert", 0),), reach)
-    padded = layer_norm(raw.astype(jnp.float32), ln_gain).astype(jnp.bfloat16)
     stream = frames[0].astype(jnp.float32)
+    normed = lax.optimization_barrier(layer_norm(stream, ln_gain).astype(jnp.bfloat16))
+    edges = layer_norm(
+        jnp.concatenate([raw[:reach], raw[reach + frame_count :]]).astype(jnp.float32), ln_gain
+    ).astype(jnp.bfloat16)
+    padded = jnp.concatenate([edges[:reach], normed, edges[reach:]])
     filtered = jnp.zeros(stream.shape, jnp.float32)
     for offset in range(taps):
         filtered = filtered + kernel[offset] * padded[offset : offset + frame_count]

time: 146 us -> 146 us (level)
  Pallas kernels: 10.2 us -> 12.2 us
    concatenate x1 -> x0, other arithmetic: 1.99 us -> none  [shards(): jnp.concatenate([w_in, w_out], axis=0)]
    pallas_call x0 -> x1, Pallas kernels: none -> 1.97 us  [stack_pair(): pl.pallas_call(body, out_shape=jax.ShapeDtypeStruct((2,) + first.shape[1:...]
    reduce_sum x2 -> x3, other arithmetic: 3.96 us -> 4.64 us  [layer_norm(): centre = jnp.mean(values, axis=-1, keepdims=True)]
where the time goes in v8:
time: 146 us; the launch traced here: 145 us
  blocking collectives  51.3 us (35%)
  waiting for transfers between devices  42.9 us (29%)
  starting transfers between devices  15.9 us (11%)
  between operations  13.7 us (9%)
  Pallas kernels  12.2 us (8%)
  other arithmetic  6.79 us (5%)
  matrix products  1.48 us (1%)
    all_to_all x1, blocking collectives, shards(): lax.all_to_all(outgoing, 'expert', split_axis=0, concat_axis=0, tiled=True)  51.3 us
    all_to_all x1, waiting for transfers between devices, shards(): lax.all_to_all(result.reshape(block.shape), 'expert', split_axis=0, conca...  39.4 us
    all_to_all x1, starting transfers between devices, shards(): lax.all_to_all(result.reshape(block.shape), 'expert', split_axis=0, conca...  10.3 us
    pallas_call x1, Pallas kernels, expert_ffn(): pl.pallas_call(body, grid=(steps,), in_specs=[pl.BlockSpec((count, width)...  10.2 us
    reduce_sum x3, other arithmetic, layer_norm(): centre = jnp.mean(values, axis=-1, keepdims=True)  4.64 us
    ppermute x1, starting transfers between devices, padded_2(): lax.ppermute(lax.slice_in_dim(block, block.shape[dim] - width, None, axis...  4.28 us
    ppermute x1, waiting for transfers between devices, padded_2(): lax.ppermute(lax.slice_in_dim(block, 0, width, axis=dim), axis, backward)  2.98 us
  transfers between devices with their start and end apart: 4, of which 3 were waited for; matrix products, arithmetic and copies ran while one was open for 5% of the time, Pallas kernels for 0%

profile of v8, /device:TPU:24, one launch (start us, length us, event | category | flops | bytes accessed | tf_op | source)
XLA Modules:
  0.0 145.4 jit_solution(14389930887998222668)
XLA Ops:
  6.5 0.0 copy-start
  6.5 0.0 copy-start.6
  6.5 0.0 copy-start.1
  6.5 0.0 all-gather.2.cloned.1.call-start
  6.5 2.0 %shard_map.100 = bf16[2,96,1536]{2,1,0:T(8,128)(2,1)} custom-call(bf16[1,96,1536]{2,1,0:T(8,128)(2,1)} %first_ref.1, bf16[1,96,1536]{2,1,0:T(8,128)(2,1)} %second_ref.1), custom_call_target="tpu_custom_call" | custom-call | tf_op jit(solution)/shard_map/pallas_call | solution.py:69
  8.5 0.0 copy-start.2
  8.5 0.0 all-gather.2.cloned.1.call-update
  8.5 0.0 copy-done
  8.6 4.3 %collective-permute-start = (bf16[15,1536]{1,0:T(8,128)(2,1)S(1)}, bf16[15,1536]{1,0:T(8,128)(2,1)S(1)}, u32[]{:S(2)}, u32[]{:S(2)}) collective-permute-start(bf16[15,1536]{1,0:T(8,128)(2,1)S(1)} %get-tuple-element.38), channel_id=1, source_target_pairs={{0,1},{1,2},{2,3},{3,4},{4,5},{5,6},{6,7},{7,8},{8,9},{9,10},{10,1... | collective-permute-start | bytes 138248 | tf_op jit(solution)/shard_map/ppermute | solution.py:16
  12.9 1.3 collective-permute-start.1
  14.2 0.0 copy-done.6
  14.2 0.1 copy.15
  14.3 0.1 eq.59
  14.4 0.2 fusion
  14.6 0.0 copy-start.3
  14.7 0.0 copy-start.4
  14.7 0.1 convert_element_type.186
  14.8 0.1 copy.18
  14.9 0.2 convert_reduce_fusion
  15.0 0.0 copy-done.1
  15.1 0.2 slice_reduce_fusion.29
  15.3 0.3 fusion.5
  15.5 0.3 slice_reduce_fusion.30
  15.9 0.0 copy-done.2
  15.9 0.3 fusion.7
  16.1 0.1 fusion.17
  16.2 0.0 collective-permute-done
  16.2 3.0 %collective-permute-done.1 = bf16[15,1536]{1,0:T(8,128)(2,1)S(1)} collective-permute-done((bf16[15,1536]{1,0:T(8,128)(2,1)S(1)}, bf16[15,1536]{1,0:T(8,128)(2,1)S(1)}, u32[]{:S(2)}, u32[]{:S(2)}) %collective-permute-start.1) | collective-permute-done | bytes 46112 | tf_op jit(solution)/shard_map/ppermute | solution.py:19
  19.2 0.1 convert_reduce_fusion.1
  19.4 0.2 fusion.53
  19.6 0.0 copy-start.5
  19.6 0.1 fusion.55
  19.7 0.0 copy-done.3
  19.7 0.0 copy-done.4
  19.7 4.3 %fusion.58 = (f32[128]{0:T(128)S(1)}, f32[128,1536]{1,0:T(8,128)S(1)}) fusion(f32[1536]{0:T(1024)S(1)} %copy-done.3, bf16[15,1536]{1,0:T(8,128)(2,1)S(1)} %get-tuple-element.41, bf16[128,1536]{1,0:T(8,128)(2,1)S(1)} %fusion.7, f32[1536]{0:T(1024)S(1)} %get-tuple-element.34, f32[1536]{0:T(1024)S(1)} %get-tuple-element.35, f32[1536]{0:T(1024)S(1)} %get-tuple-element.6, ...), kind=kLoop, calls=%fused_computation.165 | loop fusion | flops 37552000 | bytes 1868288 | tf_op jit(solution)/shard_map/reduce_sum | solution.py:75
  24.1 0.2 multiply_reduce_fusion
  24.3 0.0 copy-done.5
  24.3 0.7 convolution_convert_fusion
  25.0 51.3 %all_to_all.10 = bf16[32,16,1536]{2,1,0:T(8,128)(2,1)} all-to-all(bf16[32,16,1536]{2,1,0:T(8,128)(2,1)S(1)} %bitcast.66), channel_id=1, replica_groups=mesh['fsdp'=16,'expert'=32] {'expert'}, dimensions={0} | all-to-all | bytes 3145728 | tf_op jit(solution)/shard_map/all_to_all | solution.py:119
  76.3 0.4 all-gather.2.cloned.1.call-done.first_ref.second_ref
  76.8 10.2 %shard_map.101 = bf16[512,1536]{1,0:T(8,128)(2,1)} custom-call(bf16[512,1536]{1,0:T(8,128)(2,1)} %bitcast.68, bf16[2,1536,1536]{2,1,0:T(8,128)(2,1)} %all-gather.2.cloned.1.call-done.first_ref.second_ref, bf16[2,1536,1536]{2,1,0:T(8,128)(2,1)} %all-gather.2.cloned.1.call-done.first_ref.second_ref), custom_call_target="tpu_custom_call" | custom-call | flops 4831838208 | bytes 12582912 | tf_op jit(solution)/shard_map/pallas_call | solution.py:44
  87.0 0.0 copy-start.7
  87.0 10.3 %all-to-all-start.1 = ((bf16[32,16,1536]{2,1,0:T(8,128)(2,1)}), bf16[32,16,1536]{2,1,0:T(8,128)(2,1)S(1)}, u32[]{:S(2)}, u32[]{:S(2)}) async-start(bf16[32,16,1536]{2,1,0:T(8,128)(2,1)} %bitcast.67), calls=%async_computation.1 | async-start | bytes 3145728 | tf_op jit(solution)/shard_map/all_to_all | solution.py:122
  97.3 0.1 convert_element_type.185
  97.5 0.1 copy.17
  97.5 0.0 copy-done.7
  97.5 39.4 %all-to-all-done.1 = bf16[32,16,1536]{2,1,0:T(8,128)(2,1)S(1)} async-done(((bf16[32,16,1536]{2,1,0:T(8,128)(2,1)}), bf16[32,16,1536]{2,1,0:T(8,128)(2,1)S(1)}, u32[]{:S(2)}, u32[]{:S(2)}) %all-to-all-start.1) | async-done | bytes 1572896 | tf_op jit(solution)/shard_map/all_to_all | solution.py:122
  137.0 0.6 fusion.15
  137.6 1.0 fusion.18
  (12 shorter events, 0.1 us)
Async XLA Ops:
  6.5 2.0 %copy-start = (bf16[1,128,1536]{2,1,0:T(8,128)(2,1)S(1)}, bf16[1,128,1536]{2,1,0:T(8,128)(2,1)}, u32[]{:S(2)}) copy-start(bf16[1,128,1536]{2,1,0:T(8,128)(2,1)} %param.10) | copy-start | bytes 1179652
  6.5 7.6 %copy-start.6 = (s32[1,128,2]{1,2,0:T(2,128)S(1)}, s32[1,128,2]{1,2,0:T(2,128)}, u32[]{:S(2)}) copy-start(s32[1,128,2]{1,2,0:T(2,128)} %param.16) | copy-start | bytes 3076
  6.5 8.5 %copy-start.1 = (f32[31,1536]{1,0:T(8,128)S(1)}, f32[31,1536]{1,0:T(8,128)}, u32[]{:S(2)}) copy-start(f32[31,1536]{1,0:T(8,128)} %param.12) | copy-start | bytes 571396
  6.5 70.2 %all-gather.2.cloned.1.call-start = ((), (), s32[]{:S(2)}) async-start(), calls=%async_computation.2 | async-start | bytes 10027008 | tf_op jit(solution)/shard_map/all_gather | solution.py:90
  8.5 7.3 %copy-start.2 = (f32[1536]{0:T(1024)S(1)}, f32[1536]{0:T(1024)}, u32[]{:S(2)}) copy-start(f32[1536]{0:T(1024)} %param.11) | copy-start | bytes 18436
  8.6 7.6 %collective-permute-start = (bf16[15,1536]{1,0:T(8,128)(2,1)S(1)}, bf16[15,1536]{1,0:T(8,128)(2,1)S(1)}, u32[]{:S(2)}, u32[]{:S(2)}) collective-permute-start(bf16[15,1536]{1,0:T(8,128)(2,1)S(1)} %get-tuple-element.38), channel_id=1, source_target_pairs={{0,1},{1,2},{2,3},{3,4},{4,5},{5,6},{6,7},{7,8},{8,9},{9,10},{10,1... | collective-permute-start | bytes 138248 | tf_op jit(solution)/shard_map/ppermute | solution.py:16
  12.9 6.3 %collective-permute-start.1 = (bf16[15,1536]{1,0:T(8,128)(2,1)S(1)}, bf16[15,1536]{1,0:T(8,128)(2,1)S(1)}, u32[]{:S(2)}, u32[]{:S(2)}) collective-permute-start(bf16[15,1536]{1,0:T(8,128)(2,1)S(1)} %get-tuple-element.39), channel_id=1, source_target_pairs={{1,0},{2,1},{3,2},{4,3},{5,4},{6,5},{7,6},{8,7},{9,8},{10,9},{11,1... | collective-permute-start | bytes 138248 | tf_op jit(solution)/shard_map/ppermute | solution.py:19
  14.6 5.1 %copy-start.3 = (f32[1536]{0:T(1024)S(1)}, f32[1536]{0:T(1024)}, u32[]{:S(2)}) copy-start(f32[1536]{0:T(1024)} %param.14) | copy-start | bytes 18436
  14.7 5.1 %copy-start.4 = (f32[1536]{0:T(1024)S(1)}, f32[1536]{0:T(1024)}, u32[]{:S(2)}) copy-start(f32[1536]{0:T(1024)} %param.13) | copy-start | bytes 18436
  19.6 4.8 %copy-start.5 = (f32[1536]{0:T(1024)S(1)}, f32[1536]{0:T(1024)}, u32[]{:S(2)}) copy-start(f32[1536]{0:T(1024)} %param.15) | copy-start | bytes 18436
  87.0 10.5 %copy-start.7 = (f32[1,128,2]{1,2,0:T(2,128)S(1)}, f32[1,128,2]{1,2,0:T(2,128)}, u32[]{:S(2)}) copy-start(f32[1,128,2]{1,2,0:T(2,128)} %param.17) | copy-start | bytes 3076
  87.0 50.0 %all-to-all-start.1 = ((bf16[32,16,1536]{2,1,0:T(8,128)(2,1)}), bf16[32,16,1536]{2,1,0:T(8,128)(2,1)S(1)}, u32[]{:S(2)}, u32[]{:S(2)}) async-start(bf16[32,16,1536]{2,1,0:T(8,128)(2,1)} %bitcast.67), calls=%async_computation.1 | async-start | bytes 3145728 | tf_op jit(solution)/shard_map/all_to_all | solution.py:122
Sparse Core Ops, SparseCore 0:
  9.5 67.2 all-gather.1

commit v9 on v6

--- a/solution.py
+++ b/solution.py
@@ -23,7 +23,7 @@
 
 def expert_ffn(rows, both, step=512):
     count, width = rows.shape
-    hidden_units = both.shape[2]
+    hidden_units = both.shape[2] // 2
     steps = hidden_units // step
 
     def body(x_ref, first_ref, second_ref, out_ref, acc_ref):
@@ -47,7 +47,7 @@
         in_specs=[
             pl.BlockSpec((count, width), lambda j: (0, 0)),
             pl.BlockSpec((None, width, step), lambda j: (0, 0, j)),
-            pl.BlockSpec((None, step, width), lambda j: (1, j, 0)),
+            pl.BlockSpec((None, step, width), lambda j: (0, j, 1)),
         ],
         out_specs=pl.BlockSpec((count, width), lambda j: (0, 0)),
         out_shape=jax.ShapeDtypeStruct((count, width), jnp.bfloat16),
@@ -77,7 +77,7 @@
     experts_all = lax.axis_size("expert") * w_in.shape[0]
     capacity = 2 * picks_per * frame_count // experts_all
     slots_all = experts_all * capacity
-    both = lax.all_gather(jnp.concatenate([w_in, w_out], axis=0), "fsdp", axis=1, tiled=True)
+    both = lax.all_gather(jnp.concatenate([w_in, w_out], axis=2), "fsdp", axis=1, tiled=True)
     raw = padded_2(frames[0], (("expert", 0),), reach)
     padded = layer_norm(raw.astype(jnp.float32), ln_gain).astype(jnp.bfloat16)
     stream = frames[0].astype(jnp.float32)

time: 146 us -> 145 us (level)
  no operation moved by 1% of the time
where the time goes in v9:
time: 145 us
  blocking collectives  51.3 us (35%)
  waiting for transfers between devices  43.6 us (30%)
  starting transfers between devices  15.9 us (11%)
  between operations  13.6 us (9%)
  Pallas kernels  9.72 us (7%)
  other arithmetic  8.01 us (6%)
  matrix products  1.48 us (1%)
    all_to_all x1, blocking collectives, shards(): lax.all_to_all(outgoing, 'expert', split_axis=0, concat_axis=0, tiled=True)  51.3 us
    all_to_all x1, waiting for transfers between devices, shards(): lax.all_to_all(result.reshape(block.shape), 'expert', split_axis=0, conca...  39.4 us
    all_to_all x1, starting transfers between devices, shards(): lax.all_to_all(result.reshape(block.shape), 'expert', split_axis=0, conca...  10.3 us
    pallas_call x1, Pallas kernels, expert_ffn(): pl.pallas_call(body, grid=(steps,), in_specs=[pl.BlockSpec((count, width)...  9.72 us
    ppermute x1, starting transfers between devices, padded_2(): lax.ppermute(lax.slice_in_dim(block, block.shape[dim] - width, None, axis...  4.28 us
    reduce_sum x2, other arithmetic, layer_norm(): centre = jnp.mean(values, axis=-1, keepdims=True)  3.96 us
    ppermute x1, waiting for transfers between devices, padded_2(): lax.ppermute(lax.slice_in_dim(block, 0, width, axis=dim), axis, backward)  3.72 us
  transfers between devices with their start and end apart: 4, of which 3 were waited for; matrix products, arithmetic and copies ran while one was open for 5% of the time, Pallas kernels for 0%

profile of v9, /device:TPU:24, one launch (start us, length us, event | category | flops | bytes accessed | tf_op | source)
XLA Modules:
  0.0 144.9 jit_solution(61337833234213850)
XLA Ops:
  6.5 0.0 copy-start
  6.5 0.0 copy-start.6
  6.5 0.0 copy-start.1
  6.5 0.0 all-gather.2.cloned.1.call-start
  6.5 2.0 %pad_maximum_fusion = bf16[1,96,3072]{2,1,0:T(8,128)(2,1)} fusion(bf16[1,96,1536]{2,1,0:T(8,128)(2,1)} %param.19, bf16[1,96,1536]{2,1,0:T(8,128)(2,1)} %param.18), kind=kLoop, calls=%fused_computation.21 | loop fusion | flops 1179648 | bytes 1179648 | tf_op jit(solution)/shard_map/concatenate | solution.py:80
  8.5 0.0 copy-start.2
  8.5 0.0 all-gather.2.cloned.1.call-update
  8.5 0.0 copy-done
  8.6 0.0 copy-start.3
  8.6 0.0 copy-start.4
  8.6 4.3 %collective-permute-start = (bf16[15,1536]{1,0:T(8,128)(2,1)S(1)}, bf16[15,1536]{1,0:T(8,128)(2,1)S(1)}, u32[]{:S(2)}, u32[]{:S(2)}) collective-permute-start(bf16[15,1536]{1,0:T(8,128)(2,1)S(1)} %get-tuple-element.38), channel_id=1, source_target_pairs={{0,1},{1,2},{2,3},{3,4},{4,5},{5,6},{6,7},{7,8},{8,9},{9,10},{10,1... | collective-permute-start | bytes 138248 | tf_op jit(solution)/shard_map/ppermute | solution.py:16
  12.9 1.3 collective-permute-start.1
  14.2 0.0 copy-done.6
  14.2 0.1 copy.15
  14.3 0.1 eq.59
  14.5 0.2 fusion.2
  14.7 0.1 convert_element_type.178
  14.8 0.1 copy.18
  14.9 0.0 copy-done.1
  14.9 0.2 slice_reduce_fusion.29
  15.1 0.3 slice_reduce_fusion.30
  15.4 0.1 fusion.15
  15.5 0.0 collective-permute-done
  15.5 3.7 %collective-permute-done.1 = bf16[15,1536]{1,0:T(8,128)(2,1)S(1)} collective-permute-done((bf16[15,1536]{1,0:T(8,128)(2,1)S(1)}, bf16[15,1536]{1,0:T(8,128)(2,1)S(1)}, u32[]{:S(2)}, u32[]{:S(2)}) %collective-permute-start.1) | collective-permute-done | bytes 46112 | tf_op jit(solution)/shard_map/ppermute | solution.py:19
  19.2 0.2 convert_reduce_fusion
  19.5 0.3 fusion.3
  19.8 0.0 copy-done.2
  19.8 0.4 fusion.5
  20.3 0.0 copy-done.3
  20.3 0.0 copy-done.4
  20.3 0.0 copy-start.5
  20.3 3.7 %fusion.23 = (f32[128]{0:T(128)S(1)}, f32[128,1536]{1,0:T(8,128)S(1)}) fusion(f32[1536]{0:T(1024)S(1)} %copy-done.3, bf16[158,1536]{1,0:T(8,128)(2,1)S(1)} %fusion.5, f32[1536]{0:T(1024)S(1)} %get-tuple-element.34, f32[1536]{0:T(1024)S(1)} %get-tuple-element.35, f32[1536]{0:T(1024)S(1)} %get-tuple-element.6, f32[1536]{0:T(1024)S(1)} %get-tuple-element.7, ...), kind=kLoop, calls=%fused_computation.78 | loop fusion | flops 19857280 | bytes 13572608 | tf_op jit(solution)/shard_map/reduce_sum | solution.py:65
  24.0 0.2 multiply_reduce_fusion
  24.3 0.0 copy-done.5
  24.3 0.7 convolution_convert_fusion
  25.0 51.3 %all_to_all.10 = bf16[32,16,1536]{2,1,0:T(8,128)(2,1)} all-to-all(bf16[32,16,1536]{2,1,0:T(8,128)(2,1)S(1)} %bitcast.55), channel_id=1, replica_groups=mesh['fsdp'=16,'expert'=32] {'expert'}, dimensions={0} | all-to-all | bytes 3145728 | tf_op jit(solution)/shard_map/all_to_all | solution.py:105
  76.3 0.5 all-gather.2.cloned.1.call-done.first_ref.second_ref
  76.7 9.7 %shard_map.100 = bf16[512,1536]{1,0:T(8,128)(2,1)} custom-call(bf16[512,1536]{1,0:T(8,128)(2,1)} %bitcast.57, bf16[1,1536,3072]{2,1,0:T(8,128)(2,1)} %all-gather.2.cloned.1.call-done.first_ref.second_ref, bf16[1,1536,3072]{2,1,0:T(8,128)(2,1)} %all-gather.2.cloned.1.call-done.first_ref.second_ref), custom_call_target="tpu_custom_call" | custom-call | flops 4831838208 | bytes 12582912 | tf_op jit(solution)/shard_map/pallas_call | solution.py:44
  86.5 0.0 copy-start.7
  86.5 10.3 %all-to-all-start.1 = ((bf16[32,16,1536]{2,1,0:T(8,128)(2,1)}), bf16[32,16,1536]{2,1,0:T(8,128)(2,1)S(1)}, u32[]{:S(2)}, u32[]{:S(2)}) async-start(bf16[32,16,1536]{2,1,0:T(8,128)(2,1)} %bitcast.56), calls=%async_computation.1 | async-start | bytes 3145728 | tf_op jit(solution)/shard_map/all_to_all | solution.py:108
  96.8 0.1 convert_element_type.177
  97.0 0.1 copy.17
  97.0 0.0 copy-done.7
  97.0 39.4 %all-to-all-done.1 = bf16[32,16,1536]{2,1,0:T(8,128)(2,1)S(1)} async-done(((bf16[32,16,1536]{2,1,0:T(8,128)(2,1)}), bf16[32,16,1536]{2,1,0:T(8,128)(2,1)S(1)}, u32[]{:S(2)}, u32[]{:S(2)}) %all-to-all-start.1) | async-done | bytes 1572896 | tf_op jit(solution)/shard_map/all_to_all | solution.py:108
  136.4 0.6 fusion.13
  137.1 1.0 fusion.16
  (9 shorter events, 0.1 us)
Async XLA Ops:
  6.5 2.0 %copy-start = (bf16[1,128,1536]{2,1,0:T(8,128)(2,1)S(1)}, bf16[1,128,1536]{2,1,0:T(8,128)(2,1)}, u32[]{:S(2)}) copy-start(bf16[1,128,1536]{2,1,0:T(8,128)(2,1)} %param.10) | copy-start | bytes 1179652
  6.5 7.7 %copy-start.6 = (s32[1,128,2]{1,2,0:T(2,128)S(1)}, s32[1,128,2]{1,2,0:T(2,128)}, u32[]{:S(2)}) copy-start(s32[1,128,2]{1,2,0:T(2,128)} %param.16) | copy-start | bytes 3076
  6.5 8.4 %copy-start.1 = (f32[31,1536]{1,0:T(8,128)S(1)}, f32[31,1536]{1,0:T(8,128)}, u32[]{:S(2)}) copy-start(f32[31,1536]{1,0:T(8,128)} %param.12) | copy-start | bytes 571396
  6.5 70.2 %all-gather.2.cloned.1.call-start = ((), (), s32[]{:S(2)}) async-start(), calls=%async_computation.2 | async-start | bytes 10027008 | tf_op jit(solution)/shard_map/all_gather | solution.py:80
  8.5 11.3 %copy-start.2 = (f32[1536]{0:T(1024)S(1)}, f32[1536]{0:T(1024)}, u32[]{:S(2)}) copy-start(f32[1536]{0:T(1024)} %param.11) | copy-start | bytes 18436
  8.6 11.7 %copy-start.3 = (f32[1536]{0:T(1024)S(1)}, f32[1536]{0:T(1024)}, u32[]{:S(2)}) copy-start(f32[1536]{0:T(1024)} %param.14) | copy-start | bytes 18436
  8.6 11.7 %copy-start.4 = (f32[1536]{0:T(1024)S(1)}, f32[1536]{0:T(1024)}, u32[]{:S(2)}) copy-start(f32[1536]{0:T(1024)} %param.13) | copy-start | bytes 18436
  8.6 6.9 %collective-permute-start = (bf16[15,1536]{1,0:T(8,128)(2,1)S(1)}, bf16[15,1536]{1,0:T(8,128)(2,1)S(1)}, u32[]{:S(2)}, u32[]{:S(2)}) collective-permute-start(bf16[15,1536]{1,0:T(8,128)(2,1)S(1)} %get-tuple-element.38), channel_id=1, source_target_pairs={{0,1},{1,2},{2,3},{3,4},{4,5},{5,6},{6,7},{7,8},{8,9},{9,10},{10,1... | collective-permute-start | bytes 138248 | tf_op jit(solution)/shard_map/ppermute | solution.py:16
  12.9 6.3 %collective-permute-start.1 = (bf16[15,1536]{1,0:T(8,128)(2,1)S(1)}, bf16[15,1536]{1,0:T(8,128)(2,1)S(1)}, u32[]{:S(2)}, u32[]{:S(2)}) collective-permute-start(bf16[15,1536]{1,0:T(8,128)(2,1)S(1)} %get-tuple-element.39), channel_id=1, source_target_pairs={{1,0},{2,1},{3,2},{4,3},{5,4},{6,5},{7,6},{8,7},{9,8},{10,9},{11,1... | collective-permute-start | bytes 138248 | tf_op jit(solution)/shard_map/ppermute | solution.py:19
  20.3 4.0 %copy-start.5 = (f32[1536]{0:T(1024)S(1)}, f32[1536]{0:T(1024)}, u32[]{:S(2)}) copy-start(f32[1536]{0:T(1024)} %param.15) | copy-start | bytes 18436
  86.5 10.5 %copy-start.7 = (f32[1,128,2]{1,2,0:T(2,128)S(1)}, f32[1,128,2]{1,2,0:T(2,128)}, u32[]{:S(2)}) copy-start(f32[1,128,2]{1,2,0:T(2,128)} %param.17) | copy-start | bytes 3076
  86.5 50.0 %all-to-all-start.1 = ((bf16[32,16,1536]{2,1,0:T(8,128)(2,1)}), bf16[32,16,1536]{2,1,0:T(8,128)(2,1)S(1)}, u32[]{:S(2)}, u32[]{:S(2)}) async-start(bf16[32,16,1536]{2,1,0:T(8,128)(2,1)} %bitcast.56), calls=%async_computation.1 | async-start | bytes 3145728 | tf_op jit(solution)/shard_map/all_to_all | solution.py:108
Sparse Core Ops, SparseCore 0:
  9.5 67.2 all-gather.1

commit v10 on v9

--- a/solution.py
+++ b/solution.py
@@ -79,8 +79,12 @@
     slots_all = experts_all * capacity
     both = lax.all_gather(jnp.concatenate([w_in, w_out], axis=2), "fsdp", axis=1, tiled=True)
     raw = padded_2(frames[0], (("expert", 0),), reach)
-    padded = layer_norm(raw.astype(jnp.float32), ln_gain).astype(jnp.bfloat16)
     stream = frames[0].astype(jnp.float32)
+    normed = layer_norm(stream, ln_gain).astype(jnp.bfloat16)
+    edges = layer_norm(
+        jnp.concatenate([raw[:reach], raw[reach + frame_count :]]).astype(jnp.float32), ln_gain
+    ).astype(jnp.bfloat16)
+    padded = jnp.concatenate([edges[:reach], normed, edges[reach:]])
     filtered = jnp.zeros(stream.shape, jnp.float32)
     for offset in range(taps):
         filtered = filtered + kernel[offset] * padded[offset : offset + frame_count]

time: 145 us -> 145 us (level)
    reduce_sum x2 -> x3, other arithmetic: 3.96 us -> 4.64 us  [layer_norm(): centre = jnp.mean(values, axis=-1, keepdims=True)]
where the time goes in v10:
time: 145 us
  blocking collectives  51.3 us (35%)
  waiting for transfers between devices  42.8 us (30%)
  starting transfers between devices  15.9 us (11%)
  between operations  13.7 us (9%)
  Pallas kernels  9.72 us (7%)
  other arithmetic  8.77 us (6%)
  matrix products  1.48 us (1%)
    all_to_all x1, blocking collectives, shards(): lax.all_to_all(outgoing, 'expert', split_axis=0, concat_axis=0, tiled=True)  51.3 us
    all_to_all x1, waiting for transfers between devices, shards(): lax.all_to_all(result.reshape(block.shape), 'expert', split_axis=0, conca...  39.4 us
    all_to_all x1, starting transfers between devices, shards(): lax.all_to_all(result.reshape(block.shape), 'expert', split_axis=0, conca...  10.3 us
    pallas_call x1, Pallas kernels, expert_ffn(): pl.pallas_call(body, grid=(steps,), in_specs=[pl.BlockSpec((count, width)...  9.72 us
    reduce_sum x3, other arithmetic, layer_norm(): centre = jnp.mean(values, axis=-1, keepdims=True)  4.64 us
    ppermute x1, starting transfers between devices, padded_2(): lax.ppermute(lax.slice_in_dim(block, block.shape[dim] - width, None, axis...  4.28 us
    ppermute x1, waiting for transfers between devices, padded_2(): lax.ppermute(lax.slice_in_dim(block, 0, width, axis=dim), axis, backward)  2.98 us
  transfers between devices with their start and end apart: 4, of which 3 were waited for; matrix products, arithmetic and copies ran while one was open for 5% of the time, Pallas kernels for 0%

profile of v10, /device:TPU:24, one launch (start us, length us, event | category | flops | bytes accessed | tf_op | source)
XLA Modules:
  0.0 144.9 jit_solution(8238666251446692472)
XLA Ops:
  6.5 0.0 copy-start
  6.5 0.0 copy-start.6
  6.5 0.0 copy-start.1
  6.5 0.0 all-gather.2.cloned.1.call-start
  6.5 2.0 %pad_maximum_fusion = bf16[1,96,3072]{2,1,0:T(8,128)(2,1)} fusion(bf16[1,96,1536]{2,1,0:T(8,128)(2,1)} %param.19, bf16[1,96,1536]{2,1,0:T(8,128)(2,1)} %param.18), kind=kLoop, calls=%fused_computation.50 | loop fusion | flops 1179648 | bytes 1179648 | tf_op jit(solution)/shard_map/concatenate | solution.py:80
  8.5 0.0 copy-start.2
  8.5 0.0 all-gather.2.cloned.1.call-update
  8.5 0.0 copy-done
  8.6 4.3 %collective-permute-start = (bf16[15,1536]{1,0:T(8,128)(2,1)S(1)}, bf16[15,1536]{1,0:T(8,128)(2,1)S(1)}, u32[]{:S(2)}, u32[]{:S(2)}) collective-permute-start(bf16[15,1536]{1,0:T(8,128)(2,1)S(1)} %get-tuple-element.38), channel_id=1, source_target_pairs={{0,1},{1,2},{2,3},{3,4},{4,5},{5,6},{6,7},{7,8},{8,9},{9,10},{10,1... | collective-permute-start | bytes 138248 | tf_op jit(solution)/shard_map/ppermute | solution.py:16
  12.9 1.3 collective-permute-start.1
  14.2 0.0 copy-done.6
  14.2 0.1 copy.15
  14.3 0.1 eq.59
  14.4 0.2 fusion
  14.6 0.0 copy-start.3
  14.7 0.0 copy-start.4
  14.7 0.1 convert_element_type.186
  14.8 0.1 copy.18
  14.9 0.2 convert_reduce_fusion
  15.1 0.0 copy-done.1
  15.1 0.2 slice_reduce_fusion.29
  15.3 0.3 fusion.5
  15.5 0.3 slice_reduce_fusion.30
  15.9 0.0 copy-done.2
  15.9 0.3 fusion.7
  16.2 0.1 fusion.17
  16.2 0.0 collective-permute-done
  16.2 3.0 %collective-permute-done.1 = bf16[15,1536]{1,0:T(8,128)(2,1)S(1)} collective-permute-done((bf16[15,1536]{1,0:T(8,128)(2,1)S(1)}, bf16[15,1536]{1,0:T(8,128)(2,1)S(1)}, u32[]{:S(2)}, u32[]{:S(2)}) %collective-permute-start.1) | collective-permute-done | bytes 46112 | tf_op jit(solution)/shard_map/ppermute | solution.py:19
  19.2 0.1 convert_reduce_fusion.1
  19.4 0.2 fusion.53
  19.6 0.0 copy-start.5
  19.6 0.1 fusion.55
  19.7 0.0 copy-done.3
  19.7 0.0 copy-done.4
  19.7 4.3 %fusion.58 = (f32[128]{0:T(128)S(1)}, f32[128,1536]{1,0:T(8,128)S(1)}) fusion(f32[1536]{0:T(1024)S(1)} %copy-done.3, bf16[15,1536]{1,0:T(8,128)(2,1)S(1)} %get-tuple-element.41, bf16[128,1536]{1,0:T(8,128)(2,1)S(1)} %fusion.7, f32[1536]{0:T(1024)S(1)} %get-tuple-element.34, f32[1536]{0:T(1024)S(1)} %get-tuple-element.35, f32[1536]{0:T(1024)S(1)} %get-tuple-element.6, ...), kind=kLoop, calls=%fused_computation.166 | loop fusion | flops 37552000 | bytes 1868288 | tf_op jit(solution)/shard_map/reduce_sum | solution.py:65
  24.1 0.2 multiply_reduce_fusion
  24.3 0.0 copy-done.5
  24.3 0.7 convolution_convert_fusion
  25.0 51.3 %all_to_all.10 = bf16[32,16,1536]{2,1,0:T(8,128)(2,1)} all-to-all(bf16[32,16,1536]{2,1,0:T(8,128)(2,1)S(1)} %bitcast.66), channel_id=1, replica_groups=mesh['fsdp'=16,'expert'=32] {'expert'}, dimensions={0} | all-to-all | bytes 3145728 | tf_op jit(solution)/shard_map/all_to_all | solution.py:109
  76.3 0.4 all-gather.2.cloned.1.call-done.first_ref.second_ref
  76.7 9.7 %shard_map.100 = bf16[512,1536]{1,0:T(8,128)(2,1)} custom-call(bf16[512,1536]{1,0:T(8,128)(2,1)} %bitcast.68, bf16[1,1536,3072]{2,1,0:T(8,128)(2,1)} %all-gather.2.cloned.1.call-done.first_ref.second_ref, bf16[1,1536,3072]{2,1,0:T(8,128)(2,1)} %all-gather.2.cloned.1.call-done.first_ref.second_ref), custom_call_target="tpu_custom_call" | custom-call | flops 4831838208 | bytes 12582912 | tf_op jit(solution)/shard_map/pallas_call | solution.py:44
  86.5 0.0 copy-start.7
  86.5 10.3 %all-to-all-start.1 = ((bf16[32,16,1536]{2,1,0:T(8,128)(2,1)}), bf16[32,16,1536]{2,1,0:T(8,128)(2,1)S(1)}, u32[]{:S(2)}, u32[]{:S(2)}) async-start(bf16[32,16,1536]{2,1,0:T(8,128)(2,1)} %bitcast.67), calls=%async_computation.1 | async-start | bytes 3145728 | tf_op jit(solution)/shard_map/all_to_all | solution.py:112
  96.8 0.1 convert_element_type.185
  97.0 0.1 copy.17
  97.0 0.0 copy-done.7
  97.0 39.4 %all-to-all-done.1 = bf16[32,16,1536]{2,1,0:T(8,128)(2,1)S(1)} async-done(((bf16[32,16,1536]{2,1,0:T(8,128)(2,1)}), bf16[32,16,1536]{2,1,0:T(8,128)(2,1)S(1)}, u32[]{:S(2)}, u32[]{:S(2)}) %all-to-all-start.1) | async-done | bytes 1572896 | tf_op jit(solution)/shard_map/all_to_all | solution.py:112
  136.4 0.6 fusion.15
  137.1 1.0 fusion.18
  (12 shorter events, 0.1 us)
Async XLA Ops:
  6.5 2.0 %copy-start = (bf16[1,128,1536]{2,1,0:T(8,128)(2,1)S(1)}, bf16[1,128,1536]{2,1,0:T(8,128)(2,1)}, u32[]{:S(2)}) copy-start(bf16[1,128,1536]{2,1,0:T(8,128)(2,1)} %param.10) | copy-start | bytes 1179652
  6.5 7.6 %copy-start.6 = (s32[1,128,2]{1,2,0:T(2,128)S(1)}, s32[1,128,2]{1,2,0:T(2,128)}, u32[]{:S(2)}) copy-start(s32[1,128,2]{1,2,0:T(2,128)} %param.16) | copy-start | bytes 3076
  6.5 8.5 %copy-start.1 = (f32[31,1536]{1,0:T(8,128)S(1)}, f32[31,1536]{1,0:T(8,128)}, u32[]{:S(2)}) copy-start(f32[31,1536]{1,0:T(8,128)} %param.12) | copy-start | bytes 571396
  6.5 70.2 %all-gather.2.cloned.1.call-start = ((), (), s32[]{:S(2)}) async-start(), calls=%async_computation.2 | async-start | bytes 10027008 | tf_op jit(solution)/shard_map/all_gather | solution.py:80
  8.5 7.3 %copy-start.2 = (f32[1536]{0:T(1024)S(1)}, f32[1536]{0:T(1024)}, u32[]{:S(2)}) copy-start(f32[1536]{0:T(1024)} %param.11) | copy-start | bytes 18436
  8.6 7.6 %collective-permute-start = (bf16[15,1536]{1,0:T(8,128)(2,1)S(1)}, bf16[15,1536]{1,0:T(8,128)(2,1)S(1)}, u32[]{:S(2)}, u32[]{:S(2)}) collective-permute-start(bf16[15,1536]{1,0:T(8,128)(2,1)S(1)} %get-tuple-element.38), channel_id=1, source_target_pairs={{0,1},{1,2},{2,3},{3,4},{4,5},{5,6},{6,7},{7,8},{8,9},{9,10},{10,1... | collective-permute-start | bytes 138248 | tf_op jit(solution)/shard_map/ppermute | solution.py:16
  12.9 6.3 %collective-permute-start.1 = (bf16[15,1536]{1,0:T(8,128)(2,1)S(1)}, bf16[15,1536]{1,0:T(8,128)(2,1)S(1)}, u32[]{:S(2)}, u32[]{:S(2)}) collective-permute-start(bf16[15,1536]{1,0:T(8,128)(2,1)S(1)} %get-tuple-element.39), channel_id=1, source_target_pairs={{1,0},{2,1},{3,2},{4,3},{5,4},{6,5},{7,6},{8,7},{9,8},{10,9},{11,1... | collective-permute-start | bytes 138248 | tf_op jit(solution)/shard_map/ppermute | solution.py:19
  14.6 5.1 %copy-start.3 = (f32[1536]{0:T(1024)S(1)}, f32[1536]{0:T(1024)}, u32[]{:S(2)}) copy-start(f32[1536]{0:T(1024)} %param.14) | copy-start | bytes 18436
  14.7 5.1 %copy-start.4 = (f32[1536]{0:T(1024)S(1)}, f32[1536]{0:T(1024)}, u32[]{:S(2)}) copy-start(f32[1536]{0:T(1024)} %param.13) | copy-start | bytes 18436
  19.6 4.8 %copy-start.5 = (f32[1536]{0:T(1024)S(1)}, f32[1536]{0:T(1024)}, u32[]{:S(2)}) copy-start(f32[1536]{0:T(1024)} %param.15) | copy-start | bytes 18436
  86.5 10.5 %copy-start.7 = (f32[1,128,2]{1,2,0:T(2,128)S(1)}, f32[1,128,2]{1,2,0:T(2,128)}, u32[]{:S(2)}) copy-start(f32[1,128,2]{1,2,0:T(2,128)} %param.17) | copy-start | bytes 3076
  86.5 50.0 %all-to-all-start.1 = ((bf16[32,16,1536]{2,1,0:T(8,128)(2,1)}), bf16[32,16,1536]{2,1,0:T(8,128)(2,1)S(1)}, u32[]{:S(2)}, u32[]{:S(2)}) async-start(bf16[32,16,1536]{2,1,0:T(8,128)(2,1)} %bitcast.67), calls=%async_computation.1 | async-start | bytes 3145728 | tf_op jit(solution)/shard_map/all_to_all | solution.py:112
Sparse Core Ops, SparseCore 0:
  9.5 67.2 all-gather.1

commit v11 on v10

--- a/solution.py
+++ b/solution.py
@@ -21,13 +21,14 @@
     return block
 
 
-def expert_ffn(rows, both, step=512):
+def expert_ffn(rows, both, step=512, tiles=2):
     count, width = rows.shape
     hidden_units = both.shape[2] // 2
     steps = hidden_units // step
+    tile = count // tiles
 
     def body(x_ref, first_ref, second_ref, out_ref, acc_ref):
-        j = pl.program_id(0)
+        j = pl.program_id(1)
 
         @pl.when(j == 0)
         def _():
@@ -43,20 +44,20 @@
 
     return pl.pallas_call(
         body,
-        grid=(steps,),
+        grid=(tiles, steps),
         in_specs=[
-            pl.BlockSpec((count, width), lambda j: (0, 0)),
-            pl.BlockSpec((None, width, step), lambda j: (0, 0, j)),
-            pl.BlockSpec((None, step, width), lambda j: (0, j, 1)),
+            pl.BlockSpec((tile, width), lambda m, j: (m, 0)),
+            pl.BlockSpec((None, width, step), lambda m, j: (0, 0, j)),
+            pl.BlockSpec((None, step, width), lambda m, j: (0, j, 1)),
         ],
-        out_specs=pl.BlockSpec((count, width), lambda j: (0, 0)),
+        out_specs=pl.BlockSpec((tile, width), lambda m, j: (m, 0)),
         out_shape=jax.ShapeDtypeStruct((count, width), jnp.bfloat16),
-        scratch_shapes=[pltpu.VMEM((count, width), jnp.float32)],
-        compiler_params=pltpu.CompilerParams(dimension_semantics=("arbitrary",)),
+        scratch_shapes=[pltpu.VMEM((tile, width), jnp.float32)],
+        compiler_params=pltpu.CompilerParams(dimension_semantics=("arbitrary", "arbitrary")),
         cost_estimate=pl.CostEstimate(
             flops=4 * count * width * hidden_units,
             transcendentals=count * hidden_units,
-            bytes_accessed=2 * (2 * count * width + 2 * width * hidden_units),
+            bytes_accessed=2 * (2 * count * width + 2 * tiles * width * hidden_units),
         ),
     )(rows, both, both)
 

time: 145 us -> 148 us (1.021)
  Pallas kernels: 9.72 us -> 12.3 us
    pallas_call x1, Pallas kernels: 9.72 us -> 12.3 us  [expert_ffn(): pl.pallas_call(body, grid=(tiles, steps), in_specs=[pl.BlockSpec((tile, w...]
where the time goes in v11:
time: 148 us; the launch traced here: 147 us
  blocking collectives  51.3 us (35%)
  waiting for transfers between devices  42.8 us (29%)
  starting transfers between devices  15.9 us (11%)
  between operations  13.7 us (9%)
  Pallas kernels  12.3 us (8%)
  other arithmetic  8.77 us (6%)
  matrix products  1.48 us (1%)
    all_to_all x1, blocking collectives, shards(): lax.all_to_all(outgoing, 'expert', split_axis=0, concat_axis=0, tiled=True)  51.3 us
    all_to_all x1, waiting for transfers between devices, shards(): lax.all_to_all(result.reshape(block.shape), 'expert', split_axis=0, conca...  39.4 us
    pallas_call x1, Pallas kernels, expert_ffn(): pl.pallas_call(body, grid=(tiles, steps), in_specs=[pl.BlockSpec((tile, w...  12.3 us
    all_to_all x1, starting transfers between devices, shards(): lax.all_to_all(result.reshape(block.shape), 'expert', split_axis=0, conca...  10.3 us
    reduce_sum x3, other arithmetic, layer_norm(): centre = jnp.mean(values, axis=-1, keepdims=True)  4.64 us
    ppermute x1, starting transfers between devices, padded_2(): lax.ppermute(lax.slice_in_dim(block, block.shape[dim] - width, None, axis...  4.28 us
    ppermute x1, waiting for transfers between devices, padded_2(): lax.ppermute(lax.slice_in_dim(block, 0, width, axis=dim), axis, backward)  2.98 us
  transfers between devices with their start and end apart: 4, of which 3 were waited for; matrix products, arithmetic and copies ran while one was open for 5% of the time, Pallas kernels for 0%

profile of v11, /device:TPU:24, one launch (start us, length us, event | category | flops | bytes accessed | tf_op | source)
XLA Modules:
  0.0 147.4 jit_solution(15651644048300859830)
XLA Ops:
  6.5 0.0 copy-start
  6.5 0.0 copy-start.6
  6.5 0.0 copy-start.1
  6.5 0.0 all-gather.2.cloned.1.call-start
  6.5 2.0 %pad_maximum_fusion = bf16[1,96,3072]{2,1,0:T(8,128)(2,1)} fusion(bf16[1,96,1536]{2,1,0:T(8,128)(2,1)} %param.19, bf16[1,96,1536]{2,1,0:T(8,128)(2,1)} %param.18), kind=kLoop, calls=%fused_computation.50 | loop fusion | flops 1179648 | bytes 1179648 | tf_op jit(solution)/shard_map/concatenate | solution.py:81
  8.5 0.0 copy-start.2
  8.5 0.0 all-gather.2.cloned.1.call-update
  8.5 0.0 copy-done
  8.6 4.3 %collective-permute-start = (bf16[15,1536]{1,0:T(8,128)(2,1)S(1)}, bf16[15,1536]{1,0:T(8,128)(2,1)S(1)}, u32[]{:S(2)}, u32[]{:S(2)}) collective-permute-start(bf16[15,1536]{1,0:T(8,128)(2,1)S(1)} %get-tuple-element.38), channel_id=1, source_target_pairs={{0,1},{1,2},{2,3},{3,4},{4,5},{5,6},{6,7},{7,8},{8,9},{9,10},{10,1... | collective-permute-start | bytes 138248 | tf_op jit(solution)/shard_map/ppermute | solution.py:16
  12.9 1.3 collective-permute-start.1
  14.2 0.0 copy-done.6
  14.2 0.1 copy.15
  14.3 0.1 eq.59
  14.4 0.2 fusion
  14.6 0.0 copy-start.3
  14.7 0.0 copy-start.4
  14.7 0.1 convert_element_type.186
  14.8 0.1 copy.18
  14.9 0.2 convert_reduce_fusion
  15.1 0.0 copy-done.1
  15.1 0.2 slice_reduce_fusion.29
  15.3 0.3 fusion.5
  15.5 0.3 slice_reduce_fusion.30
  15.9 0.0 copy-done.2
  15.9 0.3 fusion.7
  16.2 0.1 fusion.17
  16.2 0.0 collective-permute-done
  16.2 3.0 %collective-permute-done.1 = bf16[15,1536]{1,0:T(8,128)(2,1)S(1)} collective-permute-done((bf16[15,1536]{1,0:T(8,128)(2,1)S(1)}, bf16[15,1536]{1,0:T(8,128)(2,1)S(1)}, u32[]{:S(2)}, u32[]{:S(2)}) %collective-permute-start.1) | collective-permute-done | bytes 46112 | tf_op jit(solution)/shard_map/ppermute | solution.py:19
  19.2 0.1 convert_reduce_fusion.1
  19.4 0.2 fusion.53
  19.6 0.0 copy-start.5
  19.6 0.1 fusion.55
  19.7 0.0 copy-done.3
  19.7 0.0 copy-done.4
  19.7 4.3 %fusion.58 = (f32[128]{0:T(128)S(1)}, f32[128,1536]{1,0:T(8,128)S(1)}) fusion(f32[1536]{0:T(1024)S(1)} %copy-done.3, bf16[15,1536]{1,0:T(8,128)(2,1)S(1)} %get-tuple-element.41, bf16[128,1536]{1,0:T(8,128)(2,1)S(1)} %fusion.7, f32[1536]{0:T(1024)S(1)} %get-tuple-element.34, f32[1536]{0:T(1024)S(1)} %get-tuple-element.35, f32[1536]{0:T(1024)S(1)} %get-tuple-element.6, ...), kind=kLoop, calls=%fused_computation.166 | loop fusion | flops 37552000 | bytes 1868288 | tf_op jit(solution)/shard_map/reduce_sum | solution.py:66
  24.1 0.2 multiply_reduce_fusion
  24.3 0.0 copy-done.5
  24.3 0.7 convolution_convert_fusion
  25.0 51.3 %all_to_all.10 = bf16[32,16,1536]{2,1,0:T(8,128)(2,1)} all-to-all(bf16[32,16,1536]{2,1,0:T(8,128)(2,1)S(1)} %bitcast.66), channel_id=1, replica_groups=mesh['fsdp'=16,'expert'=32] {'expert'}, dimensions={0} | all-to-all | bytes 3145728 | tf_op jit(solution)/shard_map/all_to_all | solution.py:110
  76.3 0.4 all-gather.2.cloned.1.call-done.first_ref.second_ref
  76.7 12.3 %shard_map.100 = bf16[512,1536]{1,0:T(8,128)(2,1)} custom-call(bf16[512,1536]{1,0:T(8,128)(2,1)} %bitcast.68, bf16[1,1536,3072]{2,1,0:T(8,128)(2,1)} %all-gather.2.cloned.1.call-done.first_ref.second_ref, bf16[1,1536,3072]{2,1,0:T(8,128)(2,1)} %all-gather.2.cloned.1.call-done.first_ref.second_ref), custom_call_target="tpu_custom_call" | custom-call | flops 4831838208 | bytes 22020096 | tf_op jit(solution)/shard_map/pallas_call | solution.py:45
  89.0 0.0 copy-start.7
  89.0 10.3 %all-to-all-start.1 = ((bf16[32,16,1536]{2,1,0:T(8,128)(2,1)}), bf16[32,16,1536]{2,1,0:T(8,128)(2,1)S(1)}, u32[]{:S(2)}, u32[]{:S(2)}) async-start(bf16[32,16,1536]{2,1,0:T(8,128)(2,1)} %bitcast.67), calls=%async_computation.1 | async-start | bytes 3145728 | tf_op jit(solution)/shard_map/all_to_all | solution.py:113
  99.3 0.1 convert_element_type.185
  99.5 0.1 copy.17
  99.6 0.0 copy-done.7
  99.6 39.4 %all-to-all-done.1 = bf16[32,16,1536]{2,1,0:T(8,128)(2,1)S(1)} async-done(((bf16[32,16,1536]{2,1,0:T(8,128)(2,1)}), bf16[32,16,1536]{2,1,0:T(8,128)(2,1)S(1)}, u32[]{:S(2)}, u32[]{:S(2)}) %all-to-all-start.1) | async-done | bytes 1572896 | tf_op jit(solution)/shard_map/all_to_all | solution.py:113
  139.0 0.6 fusion.15
  139.6 1.0 fusion.18
  (12 shorter events, 0.1 us)
Async XLA Ops:
  6.5 2.0 %copy-start = (bf16[1,128,1536]{2,1,0:T(8,128)(2,1)S(1)}, bf16[1,128,1536]{2,1,0:T(8,128)(2,1)}, u32[]{:S(2)}) copy-start(bf16[1,128,1536]{2,1,0:T(8,128)(2,1)} %param.10) | copy-start | bytes 1179652
  6.5 7.6 %copy-start.6 = (s32[1,128,2]{1,2,0:T(2,128)S(1)}, s32[1,128,2]{1,2,0:T(2,128)}, u32[]{:S(2)}) copy-start(s32[1,128,2]{1,2,0:T(2,128)} %param.16) | copy-start | bytes 3076
  6.5 8.5 %copy-start.1 = (f32[31,1536]{1,0:T(8,128)S(1)}, f32[31,1536]{1,0:T(8,128)}, u32[]{:S(2)}) copy-start(f32[31,1536]{1,0:T(8,128)} %param.12) | copy-start | bytes 571396
  6.5 70.2 %all-gather.2.cloned.1.call-start = ((), (), s32[]{:S(2)}) async-start(), calls=%async_computation.2 | async-start | bytes 10027008 | tf_op jit(solution)/shard_map/all_gather | solution.py:81
  8.5 7.3 %copy-start.2 = (f32[1536]{0:T(1024)S(1)}, f32[1536]{0:T(1024)}, u32[]{:S(2)}) copy-start(f32[1536]{0:T(1024)} %param.11) | copy-start | bytes 18436
  8.6 7.6 %collective-permute-start = (bf16[15,1536]{1,0:T(8,128)(2,1)S(1)}, bf16[15,1536]{1,0:T(8,128)(2,1)S(1)}, u32[]{:S(2)}, u32[]{:S(2)}) collective-permute-start(bf16[15,1536]{1,0:T(8,128)(2,1)S(1)} %get-tuple-element.38), channel_id=1, source_target_pairs={{0,1},{1,2},{2,3},{3,4},{4,5},{5,6},{6,7},{7,8},{8,9},{9,10},{10,1... | collective-permute-start | bytes 138248 | tf_op jit(solution)/shard_map/ppermute | solution.py:16
  12.9 6.3 %collective-permute-start.1 = (bf16[15,1536]{1,0:T(8,128)(2,1)S(1)}, bf16[15,1536]{1,0:T(8,128)(2,1)S(1)}, u32[]{:S(2)}, u32[]{:S(2)}) collective-permute-start(bf16[15,1536]{1,0:T(8,128)(2,1)S(1)} %get-tuple-element.39), channel_id=1, source_target_pairs={{1,0},{2,1},{3,2},{4,3},{5,4},{6,5},{7,6},{8,7},{9,8},{10,9},{11,1... | collective-permute-start | bytes 138248 | tf_op jit(solution)/shard_map/ppermute | solution.py:19
  14.6 5.1 %copy-start.3 = (f32[1536]{0:T(1024)S(1)}, f32[1536]{0:T(1024)}, u32[]{:S(2)}) copy-start(f32[1536]{0:T(1024)} %param.14) | copy-start | bytes 18436
  14.7 5.1 %copy-start.4 = (f32[1536]{0:T(1024)S(1)}, f32[1536]{0:T(1024)}, u32[]{:S(2)}) copy-start(f32[1536]{0:T(1024)} %param.13) | copy-start | bytes 18436
  19.6 4.8 %copy-start.5 = (f32[1536]{0:T(1024)S(1)}, f32[1536]{0:T(1024)}, u32[]{:S(2)}) copy-start(f32[1536]{0:T(1024)} %param.15) | copy-start | bytes 18436
  89.0 10.5 %copy-start.7 = (f32[1,128,2]{1,2,0:T(2,128)S(1)}, f32[1,128,2]{1,2,0:T(2,128)}, u32[]{:S(2)}) copy-start(f32[1,128,2]{1,2,0:T(2,128)} %param.17) | copy-start | bytes 3076
  89.0 50.0 %all-to-all-start.1 = ((bf16[32,16,1536]{2,1,0:T(8,128)(2,1)}), bf16[32,16,1536]{2,1,0:T(8,128)(2,1)S(1)}, u32[]{:S(2)}, u32[]{:S(2)}) async-start(bf16[32,16,1536]{2,1,0:T(8,128)(2,1)} %bitcast.67), calls=%async_computation.1 | async-start | bytes 3145728 | tf_op jit(solution)/shard_map/all_to_all | solution.py:113
Sparse Core Ops, SparseCore 0:
  9.5 67.2 all-gather.1

commit v12 on v10

--- a/solution.py
+++ b/solution.py
@@ -29,13 +29,17 @@
     def body(x_ref, first_ref, second_ref, out_ref, acc_ref):
         j = pl.program_id(0)
 
+        h = jnp.dot(x_ref[...], first_ref[...], preferred_element_type=jnp.float32)
+        h = (h / (1.0 + jnp.exp(-h))).astype(jnp.bfloat16)
+        part = jnp.dot(h, second_ref[...], preferred_element_type=jnp.float32)
+
         @pl.when(j == 0)
         def _():
-            acc_ref[...] = jnp.zeros_like(acc_ref)
+            acc_ref[...] = part
 
-        h = jnp.dot(x_ref[...], first_ref[...], preferred_element_type=jnp.float32)
-        h = (h / (1.0 + jnp.exp(-h))).astype(jnp.bfloat16)
-        acc_ref[...] += jnp.dot(h, second_ref[...], preferred_element_type=jnp.float32)
+        @pl.when(j > 0)
+        def _():
+            acc_ref[...] += part
 
         @pl.when(j == steps - 1)
         def _():

time: 145 us -> 146 us (level)
  no operation moved by 1% of the time
where the time goes in v12:
time: 146 us; the launch traced here: 145 us
  blocking collectives  51.3 us (35%)
  waiting for transfers between devices  42.8 us (29%)
  starting transfers between devices  15.9 us (11%)
  between operations  13.7 us (9%)
  Pallas kernels  10.3 us (7%)
  other arithmetic  8.77 us (6%)
  matrix products  1.48 us (1%)
    all_to_all x1, blocking collectives, shards(): lax.all_to_all(outgoing, 'expert', split_axis=0, concat_axis=0, tiled=True)  51.3 us
    all_to_all x1, waiting for transfers between devices, shards(): lax.all_to_all(result.reshape(block.shape), 'expert', split_axis=0, conca...  39.4 us
    all_to_all x1, starting transfers between devices, shards(): lax.all_to_all(result.reshape(block.shape), 'expert', split_axis=0, conca...  10.3 us
    pallas_call x1, Pallas kernels, expert_ffn(): pl.pallas_call(body, grid=(steps,), in_specs=[pl.BlockSpec((count, width)...  10.3 us
    reduce_sum x3, other arithmetic, layer_norm(): centre = jnp.mean(values, axis=-1, keepdims=True)  4.64 us
    ppermute x1, starting transfers between devices, padded_2(): lax.ppermute(lax.slice_in_dim(block, block.shape[dim] - width, None, axis...  4.28 us
    ppermute x1, waiting for transfers between devices, padded_2(): lax.ppermute(lax.slice_in_dim(block, 0, width, axis=dim), axis, backward)  2.98 us
  transfers between devices with their start and end apart: 4, of which 3 were waited for; matrix products, arithmetic and copies ran while one was open for 5% of the time, Pallas kernels for 0%

profile of v12, /device:TPU:24, one launch (start us, length us, event | category | flops | bytes accessed | tf_op | source)
XLA Modules:
  0.0 145.5 jit_solution(9961118863488716761)
XLA Ops:
  6.5 0.0 copy-start
  6.5 0.0 copy-start.6
  6.5 0.0 copy-start.1
  6.5 0.0 all-gather.2.cloned.1.call-start
  6.5 2.0 %pad_maximum_fusion = bf16[1,96,3072]{2,1,0:T(8,128)(2,1)} fusion(bf16[1,96,1536]{2,1,0:T(8,128)(2,1)} %param.19, bf16[1,96,1536]{2,1,0:T(8,128)(2,1)} %param.18), kind=kLoop, calls=%fused_computation.50 | loop fusion | flops 1179648 | bytes 1179648 | tf_op jit(solution)/shard_map/concatenate | solution.py:84
  8.5 0.0 copy-start.2
  8.5 0.0 all-gather.2.cloned.1.call-update
  8.5 0.0 copy-done
  8.6 4.3 %collective-permute-start = (bf16[15,1536]{1,0:T(8,128)(2,1)S(1)}, bf16[15,1536]{1,0:T(8,128)(2,1)S(1)}, u32[]{:S(2)}, u32[]{:S(2)}) collective-permute-start(bf16[15,1536]{1,0:T(8,128)(2,1)S(1)} %get-tuple-element.38), channel_id=1, source_target_pairs={{0,1},{1,2},{2,3},{3,4},{4,5},{5,6},{6,7},{7,8},{8,9},{9,10},{10,1... | collective-permute-start | bytes 138248 | tf_op jit(solution)/shard_map/ppermute | solution.py:16
  12.9 1.3 collective-permute-start.1
  14.2 0.0 copy-done.6
  14.2 0.1 copy.15
  14.3 0.1 eq.59
  14.4 0.2 fusion
  14.6 0.0 copy-start.3
  14.7 0.0 copy-start.4
  14.7 0.1 convert_element_type.186
  14.8 0.1 copy.18
  14.9 0.2 convert_reduce_fusion
  15.1 0.0 copy-done.1
  15.1 0.2 slice_reduce_fusion.29
  15.3 0.3 fusion.5
  15.5 0.3 slice_reduce_fusion.30
  15.9 0.0 copy-done.2
  15.9 0.3 fusion.7
  16.2 0.1 fusion.17
  16.2 0.0 collective-permute-done
  16.2 3.0 %collective-permute-done.1 = bf16[15,1536]{1,0:T(8,128)(2,1)S(1)} collective-permute-done((bf16[15,1536]{1,0:T(8,128)(2,1)S(1)}, bf16[15,1536]{1,0:T(8,128)(2,1)S(1)}, u32[]{:S(2)}, u32[]{:S(2)}) %collective-permute-start.1) | collective-permute-done | bytes 46112 | tf_op jit(solution)/shard_map/ppermute | solution.py:19
  19.2 0.1 convert_reduce_fusion.1
  19.4 0.2 fusion.53
  19.6 0.0 copy-start.5
  19.6 0.1 fusion.55
  19.7 0.0 copy-done.3
  19.7 0.0 copy-done.4
  19.7 4.3 %fusion.58 = (f32[128]{0:T(128)S(1)}, f32[128,1536]{1,0:T(8,128)S(1)}) fusion(f32[1536]{0:T(1024)S(1)} %copy-done.3, bf16[15,1536]{1,0:T(8,128)(2,1)S(1)} %get-tuple-element.41, bf16[128,1536]{1,0:T(8,128)(2,1)S(1)} %fusion.7, f32[1536]{0:T(1024)S(1)} %get-tuple-element.34, f32[1536]{0:T(1024)S(1)} %get-tuple-element.35, f32[1536]{0:T(1024)S(1)} %get-tuple-element.6, ...), kind=kLoop, calls=%fused_computation.166 | loop fusion | flops 37552000 | bytes 1868288 | tf_op jit(solution)/shard_map/reduce_sum | solution.py:69
  24.1 0.2 multiply_reduce_fusion
  24.3 0.0 copy-done.5
  24.3 0.7 convolution_convert_fusion
  25.0 51.3 %all_to_all.10 = bf16[32,16,1536]{2,1,0:T(8,128)(2,1)} all-to-all(bf16[32,16,1536]{2,1,0:T(8,128)(2,1)S(1)} %bitcast.66), channel_id=1, replica_groups=mesh['fsdp'=16,'expert'=32] {'expert'}, dimensions={0} | all-to-all | bytes 3145728 | tf_op jit(solution)/shard_map/all_to_all | solution.py:113
  76.3 0.4 all-gather.2.cloned.1.call-done.first_ref.second_ref
  76.7 10.3 %shard_map.100 = bf16[512,1536]{1,0:T(8,128)(2,1)} custom-call(bf16[512,1536]{1,0:T(8,128)(2,1)} %bitcast.68, bf16[1,1536,3072]{2,1,0:T(8,128)(2,1)} %all-gather.2.cloned.1.call-done.first_ref.second_ref, bf16[1,1536,3072]{2,1,0:T(8,128)(2,1)} %all-gather.2.cloned.1.call-done.first_ref.second_ref), custom_call_target="tpu_custom_call" | custom-call | flops 4831838208 | bytes 12582912 | tf_op jit(solution)/shard_map/pallas_call | solution.py:48
  87.1 0.0 copy-start.7
  87.1 10.3 %all-to-all-start.1 = ((bf16[32,16,1536]{2,1,0:T(8,128)(2,1)}), bf16[32,16,1536]{2,1,0:T(8,128)(2,1)S(1)}, u32[]{:S(2)}, u32[]{:S(2)}) async-start(bf16[32,16,1536]{2,1,0:T(8,128)(2,1)} %bitcast.67), calls=%async_computation.1 | async-start | bytes 3145728 | tf_op jit(solution)/shard_map/all_to_all | solution.py:116
  97.4 0.1 convert_element_type.185
  97.5 0.1 copy.17
  97.6 0.0 copy-done.7
  97.6 39.4 %all-to-all-done.1 = bf16[32,16,1536]{2,1,0:T(8,128)(2,1)S(1)} async-done(((bf16[32,16,1536]{2,1,0:T(8,128)(2,1)}), bf16[32,16,1536]{2,1,0:T(8,128)(2,1)S(1)}, u32[]{:S(2)}, u32[]{:S(2)}) %all-to-all-start.1) | async-done | bytes 1572896 | tf_op jit(solution)/shard_map/all_to_all | solution.py:116
  137.0 0.6 fusion.15
  137.6 1.0 fusion.18
  (12 shorter events, 0.1 us)
Async XLA Ops:
  6.5 2.0 %copy-start = (bf16[1,128,1536]{2,1,0:T(8,128)(2,1)S(1)}, bf16[1,128,1536]{2,1,0:T(8,128)(2,1)}, u32[]{:S(2)}) copy-start(bf16[1,128,1536]{2,1,0:T(8,128)(2,1)} %param.10) | copy-start | bytes 1179652
  6.5 7.6 %copy-start.6 = (s32[1,128,2]{1,2,0:T(2,128)S(1)}, s32[1,128,2]{1,2,0:T(2,128)}, u32[]{:S(2)}) copy-start(s32[1,128,2]{1,2,0:T(2,128)} %param.16) | copy-start | bytes 3076
  6.5 8.5 %copy-start.1 = (f32[31,1536]{1,0:T(8,128)S(1)}, f32[31,1536]{1,0:T(8,128)}, u32[]{:S(2)}) copy-start(f32[31,1536]{1,0:T(8,128)} %param.12) | copy-start | bytes 571396
  6.5 70.2 %all-gather.2.cloned.1.call-start = ((), (), s32[]{:S(2)}) async-start(), calls=%async_computation.2 | async-start | bytes 10027008 | tf_op jit(solution)/shard_map/all_gather | solution.py:84
  8.5 7.3 %copy-start.2 = (f32[1536]{0:T(1024)S(1)}, f32[1536]{0:T(1024)}, u32[]{:S(2)}) copy-start(f32[1536]{0:T(1024)} %param.11) | copy-start | bytes 18436
  8.6 7.6 %collective-permute-start = (bf16[15,1536]{1,0:T(8,128)(2,1)S(1)}, bf16[15,1536]{1,0:T(8,128)(2,1)S(1)}, u32[]{:S(2)}, u32[]{:S(2)}) collective-permute-start(bf16[15,1536]{1,0:T(8,128)(2,1)S(1)} %get-tuple-element.38), channel_id=1, source_target_pairs={{0,1},{1,2},{2,3},{3,4},{4,5},{5,6},{6,7},{7,8},{8,9},{9,10},{10,1... | collective-permute-start | bytes 138248 | tf_op jit(solution)/shard_map/ppermute | solution.py:16
  12.9 6.3 %collective-permute-start.1 = (bf16[15,1536]{1,0:T(8,128)(2,1)S(1)}, bf16[15,1536]{1,0:T(8,128)(2,1)S(1)}, u32[]{:S(2)}, u32[]{:S(2)}) collective-permute-start(bf16[15,1536]{1,0:T(8,128)(2,1)S(1)} %get-tuple-element.39), channel_id=1, source_target_pairs={{1,0},{2,1},{3,2},{4,3},{5,4},{6,5},{7,6},{8,7},{9,8},{10,9},{11,1... | collective-permute-start | bytes 138248 | tf_op jit(solution)/shard_map/ppermute | solution.py:19
  14.6 5.1 %copy-start.3 = (f32[1536]{0:T(1024)S(1)}, f32[1536]{0:T(1024)}, u32[]{:S(2)}) copy-start(f32[1536]{0:T(1024)} %param.14) | copy-start | bytes 18436
  14.7 5.1 %copy-start.4 = (f32[1536]{0:T(1024)S(1)}, f32[1536]{0:T(1024)}, u32[]{:S(2)}) copy-start(f32[1536]{0:T(1024)} %param.13) | copy-start | bytes 18436
  19.6 4.8 %copy-start.5 = (f32[1536]{0:T(1024)S(1)}, f32[1536]{0:T(1024)}, u32[]{:S(2)}) copy-start(f32[1536]{0:T(1024)} %param.15) | copy-start | bytes 18436
  87.1 10.5 %copy-start.7 = (f32[1,128,2]{1,2,0:T(2,128)S(1)}, f32[1,128,2]{1,2,0:T(2,128)}, u32[]{:S(2)}) copy-start(f32[1,128,2]{1,2,0:T(2,128)} %param.17) | copy-start | bytes 3076
  87.1 50.0 %all-to-all-start.1 = ((bf16[32,16,1536]{2,1,0:T(8,128)(2,1)}), bf16[32,16,1536]{2,1,0:T(8,128)(2,1)S(1)}, u32[]{:S(2)}, u32[]{:S(2)}) async-start(bf16[32,16,1536]{2,1,0:T(8,128)(2,1)} %bitcast.67), calls=%async_computation.1 | async-start | bytes 3145728 | tf_op jit(solution)/shard_map/all_to_all | solution.py:116
Sparse Core Ops, SparseCore 0:
  9.5 67.2 all-gather.1
